TPU v7x, 128 devices: a whole 4x4x4 slice. The times are simulated.
128 devices in a mesh: row: 16 (over y, x_lo, core), col: 8 (over z, x_hi).
Axes of the slice: x: 4 (x_hi: 2, x_lo: 2; x = x_hi * 2 + x_lo), y: 4, z: 4, core: 2. Of those that a mesh axis runs over, the one named last changes fastest.
Arguments:
- trailing: float32 [16384, 16384], P('row', 'col'), may hold values from -12 to 12, as said below
- panel: float32 [16384, 256], P('row'), may hold values from -3 to 3, as said below
Outputs:
- updated: float32 [16384, 16384], P('row', 'col')
- band_block: float32 [256, 256], replicated
Inputs may be any that keep to these rules, and one draw needn't show every extreme that they name: trailing, read in global order, equals its transpose. Read in global order, the top 256 x 256 block of panel is 2 I plus entries of magnitude at most 6 / sqrt(16384), and the rows below have entries of magnitude at most 6 / sqrt(16384).
All inputs are finite; a program needn't handle non-finite values.
Results may differ from a plain program's by a relative error of at most 0.00011.
Values sent between devices are 32-bit elements; how exact they have to be, the bound alone decides.
No kernel may reach another device: no remote copies, remote signals or barrier semaphores. Data moves between devices by JAX's collectives and lax.ppermute only.
A program may use at most 128 MiB of HBM per device.

v0:
```python
import jax
import jax.numpy as jnp
from jax import lax
from jax.sharding import PartitionSpec as P


def matmul(left, right):
    return jnp.dot(left, right, precision=lax.Precision.HIGHEST, preferred_element_type=jnp.float32)


def matmul_tn(left, right):
    return lax.dot_general(
        left,
        right,
        (((0,), (0,)), ((), ())),
        precision=lax.Precision.HIGHEST,
        preferred_element_type=jnp.float32,
    )


def matmul_nt(left, right):
    return lax.dot_general(
        left,
        right,
        (((1,), (1,)), ((), ())),
        precision=lax.Precision.HIGHEST,
        preferred_element_type=jnp.float32,
    )


def lu_unpivoted(matrix):
    order_size = matrix.shape[0]
    positions = jnp.arange(order_size)

    def eliminate(column, factors):
        below = positions > column
        column_values = lax.dynamic_slice_in_dim(factors, column, 1, 1)[:, 0]
        row_values = lax.dynamic_slice_in_dim(factors, column, 1, 0)[0]
        pivot_value = lax.dynamic_slice_in_dim(column_values, column, 1, 0)[0]
        multipliers = jnp.where(below, column_values / pivot_value, 0.0)
        pivot_row = jnp.where(below, row_values, 0.0)
        factors = factors - multipliers[:, None] * pivot_row[None, :]
        stored = jnp.where(below, multipliers, column_values)[:, None]
        return lax.dynamic_update_slice_in_dim(factors, stored, column, 1)

    factors = lax.fori_loop(0, order_size, eliminate, matrix)
    unit_lower = jnp.tril(factors, -1) + jnp.eye(order_size, dtype=matrix.dtype)
    return (unit_lower, jnp.triu(factors))


def cholesky_columns(matrix):
    order_size = matrix.shape[0]
    positions = jnp.arange(order_size)

    def factor_step(column, carry):
        remaining, factor = carry
        column_values = lax.dynamic_slice_in_dim(remaining, column, 1, 1)[:, 0]
        pivot_root = jnp.sqrt(lax.dynamic_slice_in_dim(column_values, column, 1, 0)[0])
        factor_col = jnp.where(positions >= column, column_values / pivot_root, 0.0)
        remaining = remaining - factor_col[:, None] * factor_col[None, :]
        factor = lax.dynamic_update_slice_in_dim(factor, factor_col[:, None], column, 1)
        return (remaining, factor)

    start = (matrix, jnp.zeros_like(matrix))
    return lax.fori_loop(0, order_size, factor_step, start)[1]


def inverse_lower(lower):
    order_size = lower.shape[0]
    identity = jnp.eye(order_size, dtype=jnp.float32)
    diagonal = jnp.diagonal(lower)
    nilpotent = jnp.tril(lower, -1) / diagonal[None, :]
    power = -nilpotent
    result = identity + power
    steps = max(order_size - 1, 1).bit_length() - 1
    for level in range(steps):
        power = matmul(power, power)
        result = matmul(result, identity + power)
    return result / diagonal[:, None]


def mirror(row_piece, col_count, col_index, band_size):
    group_ratio = lax.axis_size("row") // col_count
    blocks = row_piece.shape[0] // band_size
    gathered = lax.all_gather(row_piece, "row", axis=0, tiled=True)
    gathered = gathered.reshape(group_ratio, col_count, blocks, band_size, band_size)
    pieces = lax.dynamic_index_in_dim(gathered, col_index, 1, keepdims=False)
    return pieces.transpose(1, 0, 2, 3).reshape(group_ratio * row_piece.shape[0], band_size)


def shards(trailing, panel):
    col_count = lax.axis_size("col")
    row_index = lax.axis_index("row")
    col_index = lax.axis_index("col")
    band_size = panel.shape[1]
    identity = jnp.eye(band_size, dtype=jnp.float32)
    first_owner = (row_index == 0).astype(jnp.float32)
    gram_part = matmul_tn(panel, panel)
    top_part = panel[:band_size] * first_owner
    gram_total, top_rows = lax.psum((gram_part, top_part), "row")
    lower_chol = cholesky_columns(gram_total)
    chol_inverse = inverse_lower(lower_chol)
    ortho_rows = matmul_nt(panel, chol_inverse)
    ortho_top = matmul_nt(top_rows, chol_inverse)
    unit_lower, upper_tri = lu_unpivoted(identity + ortho_top)
    upper_inverse = inverse_lower(upper_tri.T).T
    unit_inverse = inverse_lower(unit_lower)
    shifted = ortho_rows.at[:band_size].add(identity * first_owner)
    reflectors = matmul(shifted, upper_inverse)
    tri_factor = matmul_nt(upper_tri, unit_inverse)
    refl_cols = mirror(reflectors, col_count, col_index, band_size)
    product_rows = lax.psum(matmul(trailing, refl_cols), "col")
    inner_gram = lax.psum(matmul_tn(reflectors, product_rows), "row")
    middle = matmul(matmul(tri_factor.T, inner_gram), tri_factor)
    update_rows = matmul(product_rows, tri_factor) - 0.5 * matmul(reflectors, middle)
    update_cols = mirror(update_rows, col_count, col_index, band_size)
    updated = trailing - matmul_nt(reflectors, update_cols) - matmul_nt(update_rows, refl_cols)
    return (updated, -lower_chol.T)


def solution(mesh):
    return jax.shard_map(
        shards,
        mesh=mesh,
        in_specs=(P("row", "col"), P("row", None)),
        out_specs=(P("row", "col"), P()),
        check_vma=False,
    )
```

profile of v0, /device:TPU:1, one launch (start us, length us, event | category | flops | bytes accessed | tf_op | source)
XLA Modules:
  0.0 1404.1 jit_solution(7878271557853717459)
XLA Ops:
  7.2 4.1 fusion.30
  11.3 1.7 slice_multiply_fusion
  13.4 121.8 %all-reduce.9.cloned.1.call-done = (f32[256,256]{1,0:T(8,128)}, f32[256,256]{1,0:T(8,128)}) async-done(((f32[256,256]{1,0:T(8,128)}, f32[256,256]{1,0:T(8,128)}), (f32[256,256]{1,0:T(8,128)}, f32[256,256]{1,0:T(8,128)})) %all-reduce.9.cloned.1.call-update) | async-done | bytes 524304 | tf_op jit(solution)/shard_map/psum | solution.py:100
  135.2 1.1 copy.23
  136.3 387.9 %while.39 = (s32[]{:T(128)}, f32[256,256]{0,1:T(8,128)S(1)}, f32[256,256]{0,1:T(8,128)S(1)}) while((s32[]{:T(128)}, f32[256,256]{0,1:T(8,128)S(1)}, f32[256,256]{0,1:T(8,128)S(1)}) %tuple.105), condition=%wide.region_2.3_spmd.clone.clone, body=%wide.region_1.0_spmd.clone.sunk.clone | while | flops 132355 | bytes 534125 | solution.py:65
  524.3 2.4 gather_fusion
  533.0 409.5 %while.40 = (s32[]{:T(128)}, f32[256,256]{0,1:T(8,128)S(1)}) while((s32[]{:T(128)}, f32[256,256]{0,1:T(8,128)S(1)}) %tuple.108), condition=%wide.region_5.6_spmd.clone.clone, body=%wide.region_4.5_spmd.clone.sunk.clone | while | flops 132355 | bytes 1058653 | solution.py:46
  533.6 0.7 reshape_select_fusion.13
  535.2 0.7 reshape_select_fusion.13
  536.8 0.7 reshape_select_fusion.13
  538.4 0.7 reshape_select_fusion.13
  540.0 0.7 reshape_select_fusion.13
  541.6 0.7 reshape_select_fusion.13
  543.2 0.7 reshape_select_fusion.13
  546.4 0.7 reshape_select_fusion.13
  548.0 0.7 reshape_select_fusion.13
  551.2 0.7 reshape_select_fusion.13
  552.8 0.7 reshape_select_fusion.13
  556.0 0.7 reshape_select_fusion.13
  557.6 0.7 reshape_select_fusion.13
  559.2 0.7 reshape_select_fusion.13
  560.8 0.7 reshape_select_fusion.13
  562.4 0.7 reshape_select_fusion.13
  942.5 2.5 gather_fusion.1
  946.4 1.0 fusion.36
  952.1 2.8 fusion.42
  955.3 2.6 gather_fusion.2
  961.2 1.1 fusion.20
  962.3 1.1 fusion.47
  963.4 84.6 %all-gather.3.cloned.1.call-done = f32[16384,256]{1,0:T(8,128)} async-done(((f32[1024,256]{1,0:T(8,128)}), f32[16384,256]{1,0:T(8,128)}) %all-gather.3.cloned.1.call-update) | async-done | bytes 16777232 | tf_op jit(solution)/shard_map/all_gather | solution.py:85
  1048.0 1.7 constant_dynamic-slice_fusion.2
  1049.9 17.2 %convolution_bitcast_fusion = f32[1024,256]{0,1:T(8,128)} fusion(f32[2048,256]{1,0:T(8,128)S(1)} %bitcast.133, f32[1024,2048]{1,0:T(8,128)} %param.8), kind=kOutput, calls=%fused_computation.43 | convolution fusion | flops 6442450944 | bytes 11534336 | tf_op jit(solution)/shard_map/dot_general | solution.py:8
  1067.6 1.4 fusion.21
  1069.0 1.4 convert_add_fusion
  1070.5 1.3 fusion.22
  1072.2 1.3 fusion.23
  1073.5 79.9 %all-reduce.5.cloned.1.call-done = f32[1024,256]{0,1:T(8,128)} async-done(((f32[1024,256]{0,1:T(8,128)}), f32[1024,256]{0,1:T(8,128)}) %all-reduce.5.cloned.1.call-update) | async-done | bytes 1048592 | tf_op jit(solution)/shard_map/psum | solution.py:112
  1153.4 3.8 fusion.49
  1157.3 4.0 fusion.48
  1161.3 117.1 %all-reduce.7.cloned.1.call-done = f32[256,256]{1,0:T(8,128)} async-done(((f32[256,256]{1,0:T(8,128)}), f32[256,256]{1,0:T(8,128)}) %all-reduce.7.cloned.1.call-update) | async-done | bytes 262160 | tf_op jit(solution)/shard_map/psum | solution.py:113
  1278.5 1.6 fusion.50
  1280.1 1.3 fusion.51
  1281.4 3.2 fusion.4
  1284.6 0.7 negate_bitcast_fusion
  1285.4 92.3 %all-gather.5.cloned.1.call-done = f32[16384,256]{1,0:T(8,128)} async-done(((f32[1024,256]{1,0:T(8,128)}), f32[16384,256]{1,0:T(8,128)}) %all-gather.5.cloned.1.call-update) | async-done | bytes 16777232 | tf_op jit(solution)/shard_map/all_gather | solution.py:85
  1377.6 1.8 constant_dynamic-slice_fusion.1
  1379.6 7.4 fusion.52
  1387.1 10.3 subtract_subtract_fusion
  (3396 shorter events, 599.4 us)
Async XLA Ops:
  7.2 128.0 %all-reduce.9.cloned.1.call-start = ((), (), s32[]{:S(2)}) async-start(), calls=%async_computation.4 | async-start | bytes 1048576 | tf_op jit(solution)/shard_map/psum | solution.py:100
  13.0 1035.0 %all-gather.3.cloned.1.call-start = ((), (), s32[]{:S(2)}) async-start(), calls=%async_computation | async-start | bytes 17825792 | tf_op jit(solution)/shard_map/all_gather | solution.py:85
  136.3 396.2 %copy-start.6 = (f32[256,256]{1,0:T(8,128)S(1)}, f32[256,256]{1,0:T(8,128)}, u32[]{:S(2)}) copy-start(f32[256,256]{1,0:T(8,128)} %get-tuple-element.275) | copy-start | bytes 786436
  524.2 5.5 copy-start.3
  530.0 416.3 %copy-start.1 = (f32[1024,256]{1,0:T(8,128)S(1)}, f32[1024,256]{1,0:T(8,128)}, u32[]{:S(2)}) copy-start(f32[1024,256]{1,0:T(8,128)} %param.9) | copy-start | bytes 3145732
  955.0 198.4 %all-reduce.5.cloned.1.call-start = ((), (), s32[]{:S(2)}) async-start(), calls=%async_computation.1 | async-start | bytes 2097152 | tf_op jit(solution)/shard_map/psum | solution.py:112
  961.2 1.1 copy-start.5
  1049.9 103.6 %copy-start = (f32[1024,256]{1,0:T(8,128)S(1)}, f32[1024,256]{1,0:T(8,128)}, u32[]{:S(2)}) copy-start(f32[1024,256]{1,0:T(8,128)} %fusion.42) | copy-start | bytes 3145732
  1067.2 211.3 %all-reduce.7.cloned.1.call-start = ((), (), s32[]{:S(2)}) async-start(), calls=%async_computation.2 | async-start | bytes 524288 | tf_op jit(solution)/shard_map/psum | solution.py:113
  1073.5 211.1 %copy-start.4 = (f32[256,256]{0,1:T(8,128)S(1)}, f32[256,256]{0,1:T(8,128)}, u32[]{:S(2)}) copy-start(f32[256,256]{0,1:T(8,128)} %copy-done.3) | copy-start | bytes 786436
  1157.2 220.4 %all-gather.5.cloned.1.call-start = ((), (), s32[]{:S(2)}) async-start(), calls=%async_computation.3 | async-start | bytes 17825792 | tf_op jit(solution)/shard_map/all_gather | solution.py:85
  1379.6 7.5 slice-start
  1379.6 7.5 copy-start.2
  1379.6 7.4 slice-start.1
Sparse Core Ops, SparseCore 0:
  13.1 122.0 all-reduce.8
  955.1 92.8 all-gather.2
  1067.3 86.1 all-reduce.4
  1157.4 121.0 all-reduce.6
  1284.8 92.8 all-gather.4
where the time goes:
time: 1420 us; the launch traced here: 1400 us
  waiting for transfers between devices  496 us (35%)
  local copies, waits for them, and re-layouts  370 us (26%)
  other arithmetic  238 us (17%)
  loops' own time  205 us (14%)
  matrix products  79.8 us (6%)
  between operations  14.6 us (1%)
    another operation x1, loops' own time, cholesky_columns(): return lax.fori_loop(0, order_size, factor_step, start)[1]  191 us
    all_gather x2, waiting for transfers between devices, mirror(): gathered = lax.all_gather(row_piece, 'row', axis=0, tiled=True)  177 us
    select_n x256, other arithmetic, eliminate(): stored = jnp.where(below, multipliers, column_values)[:, None]  168 us
    dynamic_slice x256, local copies, waits for them, and re-layouts, factor_step(): lax.dynamic_slice_in_dim(column_values, column, 1, 0)[0]  151 us
    dynamic_slice x256, local copies, waits for them, and re-layouts, eliminate(): pivot_value = lax.dynamic_slice_in_dim(column_values, column, 1, 0)[0]  151 us
    psum x1, waiting for transfers between devices, shards(): gram_total, top_rows = lax.psum((gram_part, top_part), 'row')  122 us
    psum x1, waiting for transfers between devices, shards(): inner_gram = lax.psum(matmul_tn(reflectors, product_rows), 'row')  117 us
    psum x1, waiting for transfers between devices, shards(): product_rows = lax.psum(matmul(trailing, refl_cols), 'col')  79.9 us
  transfers between devices with their start and end apart: 5, of which 5 were waited for; matrix products, arithmetic and copies ran while one was open for 1% of the time, Pallas kernels for 0%

commit v1 on v0

v1 whole, which is shorter than its diff:
```python
import jax
import jax.numpy as jnp
from jax import lax
from jax.experimental import pallas as pl
from jax.sharding import PartitionSpec as P

_INTERPRET = False
_CHUNK = 16


def matmul(left, right):
    return jnp.dot(left, right, precision=lax.Precision.HIGHEST, preferred_element_type=jnp.float32)


def matmul_tn(left, right):
    return lax.dot_general(
        left,
        right,
        (((0,), (0,)), ((), ())),
        precision=lax.Precision.HIGHEST,
        preferred_element_type=jnp.float32,
    )


def matmul_nt(left, right):
    return lax.dot_general(
        left,
        right,
        (((1,), (1,)), ((), ())),
        precision=lax.Precision.HIGHEST,
        preferred_element_type=jnp.float32,
    )


def _elim_kernel(m_ref, f_ref, r_ref):
    n = m_ref.shape[0]
    f_ref[...] = m_ref[...]
    ri = lax.broadcasted_iota(jnp.int32, (n, n), 0)
    ci = lax.broadcasted_iota(jnp.int32, (n, n), 1)
    r_ref[...] = jnp.where(ri == ci, 1.0, 0.0).astype(jnp.float32)
    for chunk in range(n // _CHUNK):
        r0 = chunk * _CHUNK
        c0 = (r0 // 128) * 128
        rc1 = min(n, ((r0 + _CHUNK - 1) // 128 + 1) * 128)
        nr = n - r0
        nc = n - c0

        def step(j, carry, r0=r0, c0=c0, rc1=rc1, nr=nr, nc=nc):
            f = f_ref[r0:, c0:]
            rows = lax.broadcasted_iota(jnp.int32, (nr, nc), 0) + r0
            row_j = jnp.sum(jnp.where(rows[:_CHUNK] == j, f[:_CHUNK], 0.0), axis=0, keepdims=True)
            lanes = lax.broadcasted_iota(jnp.int32, (nr, nc), 1) + c0
            lanes_row = lax.broadcasted_iota(jnp.int32, (1, nc), 1) + c0
            rows_col = lax.broadcasted_iota(jnp.int32, (nr, 1), 0) + r0
            col_j = jnp.sum(jnp.where(lanes == j, f, 0.0), axis=1, keepdims=True)
            pivot = jnp.sum(jnp.where(lanes_row == j, row_j, 0.0), axis=1, keepdims=True)
            mult = jnp.where(rows_col > j, col_j / pivot, 0.0)
            upd = jnp.where(lanes_row > j, row_j, 0.0)
            f = f - mult * upd
            f = jnp.where((lanes == j) & (rows > j), mult, f)
            f_ref[r0:, c0:] = f
            r_now = r_ref[r0:, :rc1]
            r_rows = lax.broadcasted_iota(jnp.int32, (_CHUNK, rc1), 0) + r0
            r_row = jnp.sum(jnp.where(r_rows == j, r_now[:_CHUNK], 0.0), axis=0, keepdims=True)
            r_ref[r0:, :rc1] = r_now - mult * r_row
            return carry

        lax.fori_loop(r0, r0 + _CHUNK, step, 0)


def eliminate(stack):
    count, n, _ = stack.shape
    spec = pl.BlockSpec((None, n, n), lambda b: (b, 0, 0))
    return pl.pallas_call(
        _elim_kernel,
        grid=(count,),
        in_specs=[spec],
        out_specs=[spec, spec],
        out_shape=[jax.ShapeDtypeStruct(stack.shape, jnp.float32)] * 2,
        interpret=_INTERPRET,
    )(stack)


def mirror(row_piece, col_count, col_index, band_size):
    group_ratio = lax.axis_size("row") // col_count
    blocks = row_piece.shape[0] // band_size
    gathered = lax.all_gather(row_piece, "row", axis=0, tiled=True)
    gathered = gathered.reshape(group_ratio, col_count, blocks, band_size, band_size)
    pieces = lax.dynamic_index_in_dim(gathered, col_index, 1, keepdims=False)
    return pieces.transpose(1, 0, 2, 3).reshape(group_ratio * row_piece.shape[0], band_size)


def small_factors(gram_total, top_rows):
    band_size = gram_total.shape[0]
    identity = jnp.eye(band_size, dtype=jnp.float32)
    gram_f, gram_r = eliminate(gram_total[None])
    gram_f = gram_f[0]
    scale = 1.0 / jnp.sqrt(jnp.diagonal(gram_f))
    chol_t = scale[:, None] * jnp.triu(gram_f)
    chol_inverse = scale[:, None] * gram_r[0]
    ortho_top = matmul_nt(top_rows, chol_inverse)
    shifted_top = identity + ortho_top
    lu_f, lu_r = eliminate(jnp.stack([shifted_top, shifted_top.T]))
    upper_tri = jnp.triu(lu_f[0])
    unit_inverse = lu_r[0]
    upper_inverse = lu_r[1].T / jnp.diagonal(lu_f[1])[None, :]
    tri_factor = matmul_nt(upper_tri, unit_inverse)
    right = matmul_tn(chol_inverse, upper_inverse)
    return chol_t, right, upper_inverse, tri_factor


def shards(trailing, panel):
    col_count = lax.axis_size("col")
    row_index = lax.axis_index("row")
    col_index = lax.axis_index("col")
    band_size = panel.shape[1]
    first_owner = (row_index == 0).astype(jnp.float32)
    gram_part = matmul_tn(panel, panel)
    top_part = panel[:band_size] * first_owner
    gram_total, top_rows = lax.psum((gram_part, top_part), "row")
    chol_t, right, upper_inverse, tri_factor = small_factors(gram_total, top_rows)
    reflectors = matmul(panel, right)
    reflectors = reflectors.at[:band_size].add(upper_inverse * first_owner)
    refl_cols = mirror(reflectors, col_count, col_index, band_size)
    product_rows = lax.psum(matmul(trailing, refl_cols), "col")
    inner_gram = lax.psum(matmul_tn(reflectors, product_rows), "row")
    middle = matmul(matmul(tri_factor.T, inner_gram), tri_factor)
    update_rows = matmul(product_rows, tri_factor) - 0.5 * matmul(reflectors, middle)
    update_cols = mirror(update_rows, col_count, col_index, band_size)
    updated = trailing - matmul_nt(reflectors, update_cols) - matmul_nt(update_rows, refl_cols)
    return (updated, -chol_t)


def solution(mesh):
    return jax.shard_map(
        shards,
        mesh=mesh,
        in_specs=(P("row", "col"), P("row", None)),
        out_specs=(P("row", "col"), P()),
        check_vma=False,
    )
```

time: 1420 us -> 735 us (0.52)
  local copies, waits for them, and re-layouts: 370 us -> 34.7 us
  other arithmetic: 238 us -> 4.45 us
  loops' own time: 205 us -> 0 us
  Pallas kernels: 0 us -> 100 us
  matrix products: 79.8 us -> 65.1 us
    dynamic_slice x512 -> x0, local copies, waits for them, and re-layouts: 302 us -> none  [the longest x256 151 us: factor_step(): lax.dynamic_slice_in_dim(column_values, column, 1, 0)[0]]
    another operation x2 -> x0, loops' own time: 205 us -> none  [the longest x1 191 us: cholesky_columns(): return lax.fori_loop(0, order_size, factor_step, start)[1]]
    select_n x1024 -> x0, other arithmetic: 176 us -> none  [the longest x256 168 us: eliminate(): stored = jnp.where(below, multipliers, column_values)[:, None]]
    pallas_call x0 -> x2, Pallas kernels: none -> 100 us  [eliminate(): pl.pallas_call(_elim_kernel, grid=(count,), in_specs=[spec], out_specs=[s...]
    sub x512 -> x0, other arithmetic: 57.3 us -> none  [the longest x256 28.7 us: factor_step(): remaining = remaining - factor_col[:, None] * factor_col[None, :]]
    while x258 -> x0, local copies, waits for them, and re-layouts: 33.1 us -> none
    dynamic_update_slice x512 -> x0, local copies, waits for them, and re-layouts: 22 us -> none  [the longest x256 11 us: eliminate(): return lax.dynamic_update_slice_in_dim(factors, stored, column, 1)]
    dot_general x48 -> x6, matrix products: 51.4 us -> 29.5 us  [matmul(): jnp.dot(left, right, precision=lax.Precision.HIGHEST, preferred_element_t...]
where the time goes in v1:
time: 735 us; the launch traced here: 728 us
  waiting for transfers between devices  508 us (69%)
  Pallas kernels  100 us (14%)
  matrix products  65.1 us (9%)
  local copies, waits for them, and re-layouts  34.7 us (5%)
  between operations  14.4 us (2%)
    all_gather x2, waiting for transfers between devices, mirror(): gathered = lax.all_gather(row_piece, 'row', axis=0, tiled=True)  185 us
    psum x1, waiting for transfers between devices, shards(): gram_total, top_rows = lax.psum((gram_part, top_part), 'row')  122 us
    psum x1, waiting for transfers between devices, shards(): inner_gram = lax.psum(matmul_tn(reflectors, product_rows), 'row')  117 us
    pallas_call x2, Pallas kernels, eliminate(): pl.pallas_call(_elim_kernel, grid=(count,), in_specs=[spec], out_specs=[s...  100 us
    psum x1, waiting for transfers between devices, shards(): product_rows = lax.psum(matmul(trailing, refl_cols), 'col')  84.1 us
    dot_general x6, matrix products, matmul(): jnp.dot(left, right, precision=lax.Precision.HIGHEST, preferred_element_t...  29.5 us
    dot_general x4, matrix products, matmul_nt(): lax.dot_general(left, right, (((1,), (1,)), ((), ())), precision=lax.Prec...  26.7 us
    reshape x1, local copies, waits for them, and re-layouts, mirror(): gathered.reshape(group_ratio, col_count, blocks, band_size, band_size)  20.4 us
  transfers between devices with their start and end apart: 5, of which 5 were waited for; matrix products, arithmetic and copies ran while one was open for 1% of the time, Pallas kernels for 0%

profile of v1, /device:TPU:1, one launch (start us, length us, event | category | flops | bytes accessed | tf_op | source)
XLA Modules:
  0.0 727.7 jit_solution(2018767468457234155)
XLA Ops:
  7.2 0.0 copy-start.2
  7.2 0.0 all-reduce.9.cloned.1.call-start
  7.2 4.2 convolution_bitcast_fusion.1
  11.4 1.7 slice_multiply_fusion
  13.1 0.0 all-reduce.9.cloned.1.call-update
  13.1 0.0 all-gather.3.cloned.1.call-start
  13.2 122.1 %all-reduce.9.cloned.1.call-done = (f32[1,256,256]{2,1,0:T(8,128)}, f32[256,256]{1,0:T(8,128)}) async-done(((f32[1,256,256]{2,1,0:T(8,128)}, f32[256,256]{1,0:T(8,128)}), (f32[1,256,256]{2,1,0:T(8,128)}, f32[256,256]{1,0:T(8,128)})) %all-reduce.9.cloned.1.call-update) | async-done | bytes 524304 | tf_op jit(solution)/shard_map/psum | solution.py:120
  135.3 34.0 %shard_map.41 = (f32[1,256,256]{2,1,0:T(8,128)}, f32[1,256,256]{2,1,0:T(8,128)}) custom-call(f32[1,256,256]{2,1,0:T(8,128)} %get-tuple-element.22.m_ref), custom_call_target="tpu_custom_call" | custom-call | tf_op jit(solution)/shard_map/pallas_call | solution.py:74
  169.3 2.6 gather_fusion
  171.9 1.5 fusion.11
  173.4 0.1 copy.5
  173.6 0.8 pad_maximum_fusion.m_ref
  174.4 66.3 %shard_map.42 = (f32[2,256,256]{2,1,0:T(8,128)}, f32[2,256,256]{2,1,0:T(8,128)}) custom-call(f32[2,256,256]{2,1,0:T(8,128)} %pad_maximum_fusion.m_ref), custom_call_target="tpu_custom_call" | custom-call | tf_op jit(solution)/shard_map/pallas_call | solution.py:74
  240.8 1.0 slice_bitcast_fusion
  241.7 2.3 gather_fusion.1
  244.1 1.7 fusion.10
  245.8 1.9 fusion.17
  247.7 0.1 copy.10
  247.8 1.1 fusion.2
  248.8 1.0 copy-done
  249.8 0.0 all-gather.3.cloned.1.call-update
  249.9 0.2 all-reduce.5.cloned.1.call-start
  250.1 92.8 %all-gather.3.cloned.1.call-done = f32[16384,256]{0,1:T(8,128)} async-done(((f32[1024,256]{0,1:T(8,128)}), f32[16384,256]{0,1:T(8,128)}) %all-gather.3.cloned.1.call-update) | async-done | bytes 16777232 | tf_op jit(solution)/shard_map/all_gather | solution.py:87
  342.9 20.4 %reshape.70 = f32[2,8,4,256,256]{3,2,1,0,4:T(4,128)} reshape(f32[16384,256]{0,1:T(8,128)} %all-gather.3.cloned.1.call-done) | data formatting | bytes 33554432 | tf_op jit(solution)/shard_map/reshape | solution.py:88
  363.3 3.3 constant_dynamic-slice_fusion.1
  366.6 2.0 copy.6
  368.6 16.6 %convolution_bitcast_fusion = f32[1024,256]{0,1:T(8,128)} fusion(f32[2048,256]{1,0:T(8,128)S(1)} %bitcast.75, f32[1024,2048]{1,0:T(8,128)} %param.4), kind=kOutput, calls=%fused_computation.3 | convolution fusion | flops 6442450944 | bytes 11534336 | tf_op jit(solution)/shard_map/dot_general | solution.py:12
  385.2 0.0 all-reduce.5.cloned.1.call-update
  385.3 0.0 all-reduce.7.cloned.1.call-start
  385.3 2.2 fusion.3
  387.5 84.1 %all-reduce.5.cloned.1.call-done = f32[1024,256]{0,1:T(8,128)} async-done(((f32[1024,256]{0,1:T(8,128)}), f32[1024,256]{0,1:T(8,128)}) %all-reduce.5.cloned.1.call-update) | async-done | bytes 1048592 | tf_op jit(solution)/shard_map/psum | solution.py:125
  471.6 3.0 fusion.19
  474.6 0.0 all-reduce.7.cloned.1.call-update
  474.6 0.3 all-gather.5.cloned.1.call-start
  474.8 4.0 fusion.18
  478.9 116.9 %all-reduce.7.cloned.1.call-done = f32[256,256]{1,0:T(8,128)} async-done(((f32[256,256]{1,0:T(8,128)}), f32[256,256]{1,0:T(8,128)}) %all-reduce.7.cloned.1.call-update) | async-done | bytes 262160 | tf_op jit(solution)/shard_map/psum | solution.py:126
  595.8 1.6 fusion.20
  597.4 1.3 fusion.21
  598.8 4.0 fusion
  602.8 0.0 all-gather.5.cloned.1.call-update
  602.8 0.8 multiply_negate_fusion
  603.6 92.1 %all-gather.5.cloned.1.call-done = f32[16384,256]{1,0:T(8,128)} async-done(((f32[1024,256]{1,0:T(8,128)}), f32[16384,256]{1,0:T(8,128)}) %all-gather.5.cloned.1.call-update) | async-done | bytes 16777232 | tf_op jit(solution)/shard_map/all_gather | solution.py:87
  695.8 1.7 constant_dynamic-slice_fusion
  697.5 0.1 copy.7
  697.7 0.0 slice-start
  697.7 0.0 copy-start.3
  697.7 13.5 %fusion.22 = f32[1024,2048]{1,0:T(8,128)S(1)} fusion(f32[1024,256]{0,1:T(8,128)S(1)} %copy-done.1, f32[2048,256]{1,0:T(8,128)S(1)} %bitcast.77), kind=kOutput, calls=%fused_computation.45 | convolution fusion | flops 6442450944 | bytes 11534336 | tf_op jit(solution)/shard_map/dot_general | solution.py:26
  711.2 9.5 %subtract_subtract_fusion = f32[1024,2048]{1,0:T(8,128)} fusion(f32[1024,2048]{1,0:T(8,128)S(1)} %bitcast.74, f32[1024,2048]{1,0:T(8,128)S(1)} %fusion.22, f32[1024,256]{1,0:T(8,128)S(1)} %copy-done.3, f32[2048,256]{1,0:T(8,128)S(1)} %bitcast.76), kind=kOutput, calls=%fused_computation.2 | convolution fusion | flops 6446645248 | bytes 28311552 | tf_op jit(solution)/shard_map/dot_general | solution.py:26
  (15 shorter events, 0.1 us)
Async XLA Ops:
  7.2 238.7 %copy-start.2 = (f32[1024,256]{1,0:T(8,128)S(1)}, f32[1024,256]{1,0:T(8,128)}, u32[]{:S(2)}) copy-start(f32[1024,256]{1,0:T(8,128)} %param.5) | copy-start | bytes 3145732
  7.2 128.1 %all-reduce.9.cloned.1.call-start = ((), (), s32[]{:S(2)}) async-start(), calls=%async_computation.4 | async-start | bytes 1048576 | tf_op jit(solution)/shard_map/psum | solution.py:120
  13.1 329.8 %all-gather.3.cloned.1.call-start = ((), (), s32[]{:S(2)}) async-start(), calls=%async_computation | async-start | bytes 17825792 | tf_op jit(solution)/shard_map/all_gather | solution.py:87
  248.8 1.0 copy-start
  249.9 221.7 %all-reduce.5.cloned.1.call-start = ((), (), s32[]{:S(2)}) async-start(), calls=%async_computation.1 | async-start | bytes 2097152 | tf_op jit(solution)/shard_map/psum | solution.py:125
  366.6 105.0 %copy-start.1 = (f32[1024,256]{0,1:T(8,128)S(1)}, f32[1024,256]{0,1:T(8,128)}, u32[]{:S(2)}) copy-start(f32[1024,256]{0,1:T(8,128)} %copy-done) | copy-start | bytes 3145732
  385.2 217.5 %copy-start.4 = (f32[1,256,256]{2,1,0:T(8,128)S(1)}, f32[1,256,256]{2,1,0:T(8,128)}, u32[]{:S(2)}) copy-start(f32[1,256,256]{2,1,0:T(8,128)} %get-tuple-element.18) | copy-start | bytes 786436
  385.3 210.5 %all-reduce.7.cloned.1.call-start = ((), (), s32[]{:S(2)}) async-start(), calls=%async_computation.2 | async-start | bytes 524288 | tf_op jit(solution)/shard_map/psum | solution.py:126
  474.6 221.2 %all-gather.5.cloned.1.call-start = ((), (), s32[]{:S(2)}) async-start(), calls=%async_computation.3 | async-start | bytes 17825792 | tf_op jit(solution)/shard_map/all_gather | solution.py:87
  697.7 13.5 %slice-start = ((s8[8388608]{0:T(1024)(128)(4,1)}), s8[4194304]{0:T(1024)(128)(4,1)S(1)}, s32[]{:S(2)}) async-start(s8[8388608]{0:T(1024)(128)(4,1)} %bitcast.73), calls=%async_computation.5 | async-start | bytes 8388608
  697.7 13.5 %copy-start.3 = (f32[1024,256]{1,0:T(8,128)S(1)}, f32[1024,256]{1,0:T(8,128)}, u32[]{:S(2)}) copy-start(f32[1024,256]{1,0:T(8,128)} %fusion) | copy-start | bytes 3145732
  697.7 13.5 %slice-start.1 = ((s8[8388608]{0:T(1024)(128)(4,1)}), s8[4194304]{0:T(1024)(128)(4,1)S(1)}, s32[]{:S(2)}) async-start(s8[8388608]{0:T(1024)(128)(4,1)} %bitcast.73), calls=%async_computation.6 | async-start | bytes 8388608
Sparse Core Ops, SparseCore 0:
  13.2 122.0 all-reduce.8
  250.0 92.8 all-gather.2
  385.4 86.1 all-reduce.4
  474.7 121.0 all-reduce.6
  602.9 92.8 all-gather.4

commit v2 on v1

--- a/solution.py
+++ b/solution.py
@@ -81,13 +81,49 @@
     )(stack)
 
 
-def mirror(row_piece, col_count, col_index, band_size):
-    group_ratio = lax.axis_size("row") // col_count
+def _xor_pairs(count, bit):
+    return [(i, i ^ bit) for i in range(count)]
+
+
+def psum_doubling(value, axis):
+    count = lax.axis_size(axis)
+    bit = 1
+    while bit < count:
+        value = value + lax.ppermute(value, axis, _xor_pairs(count, bit))
+        bit *= 2
+    return value
+
+
+def mirror_tree(row_piece, band_size):
+    row_count = lax.axis_size("row")
+    col_count = lax.axis_size("col")
+    assert row_count == 2 * col_count
+    row_index = lax.axis_index("row")
+    col_index = lax.axis_index("col")
+    piece = row_piece
+    bit = 1
+    while bit < col_count:
+        pairs = []
+        receivers = []
+        for c in range(col_count):
+            for r in range(row_count):
+                if ((r ^ c) & (col_count - 1)) & ~(bit - 1) == 0:
+                    pairs.append((r * col_count + c, (r ^ bit) * col_count + c))
+                    receivers.append((r ^ bit) * col_count + c)
+        received = lax.ppermute(piece, ("row", "col"), pairs)
+        me = row_index * col_count + col_index
+        is_receiver = jnp.zeros((), jnp.bool_)
+        for dev in receivers:
+            is_receiver = is_receiver | (me == dev)
+        piece = jnp.where(is_receiver, received, piece)
+        bit *= 2
+    other = lax.ppermute(piece, "row", _xor_pairs(row_count, col_count))
+    high = row_index >= col_count
+    first = jnp.where(high, other, piece)
+    second = jnp.where(high, piece, other)
     blocks = row_piece.shape[0] // band_size
-    gathered = lax.all_gather(row_piece, "row", axis=0, tiled=True)
-    gathered = gathered.reshape(group_ratio, col_count, blocks, band_size, band_size)
-    pieces = lax.dynamic_index_in_dim(gathered, col_index, 1, keepdims=False)
-    return pieces.transpose(1, 0, 2, 3).reshape(group_ratio * row_piece.shape[0], band_size)
+    stacked = jnp.stack([first, second]).reshape(2, blocks, band_size, row_piece.shape[1])
+    return stacked.transpose(1, 0, 2, 3).reshape(2 * row_piece.shape[0], row_piece.shape[1])
 
 
 def small_factors(gram_total, top_rows):
@@ -110,24 +146,30 @@
 
 
 def shards(trailing, panel):
-    col_count = lax.axis_size("col")
     row_index = lax.axis_index("row")
     col_index = lax.axis_index("col")
     band_size = panel.shape[1]
     first_owner = (row_index == 0).astype(jnp.float32)
+    first_col = (col_index == 0).astype(jnp.float32)
     gram_part = matmul_tn(panel, panel)
     top_part = panel[:band_size] * first_owner
-    gram_total, top_rows = lax.psum((gram_part, top_part), "row")
+    stacked = psum_doubling(jnp.concatenate([gram_part, top_part]), "row")
+    gram_total = stacked[:band_size]
+    top_rows = stacked[band_size:]
+    panel_late, gram_total = lax.optimization_barrier((panel, gram_total))
+    panel_cols = mirror_tree(panel_late, band_size)
     chol_t, right, upper_inverse, tri_factor = small_factors(gram_total, top_rows)
-    reflectors = matmul(panel, right)
-    reflectors = reflectors.at[:band_size].add(upper_inverse * first_owner)
-    refl_cols = mirror(reflectors, col_count, col_index, band_size)
-    product_rows = lax.psum(matmul(trailing, refl_cols), "col")
-    inner_gram = lax.psum(matmul_tn(reflectors, product_rows), "row")
+    refl_rows = matmul(panel, right)
+    refl_rows = refl_rows.at[:band_size].add(upper_inverse * first_owner)
+    refl_cols = matmul(panel_cols, right)
+    refl_cols = refl_cols.at[:band_size].add(upper_inverse * first_col)
+    product_rows = psum_doubling(matmul(trailing, refl_cols), "col")
+    inner_gram = psum_doubling(matmul_tn(refl_rows, product_rows), "row")
+    product_cols = mirror_tree(product_rows, band_size)
     middle = matmul(matmul(tri_factor.T, inner_gram), tri_factor)
-    update_rows = matmul(product_rows, tri_factor) - 0.5 * matmul(reflectors, middle)
-    update_cols = mirror(update_rows, col_count, col_index, band_size)
-    updated = trailing - matmul_nt(reflectors, update_cols) - matmul_nt(update_rows, refl_cols)
+    update_rows = matmul(product_rows, tri_factor) - 0.5 * matmul(refl_rows, middle)
+    update_cols = matmul(product_cols, tri_factor) - 0.5 * matmul(refl_cols, middle)
+    updated = trailing - matmul_nt(refl_rows, update_cols) - matmul_nt(update_rows, refl_cols)
     return (updated, -chol_t)
 
 

time: 735 us -> 441 us (0.60)
  waiting for transfers between devices: 508 us -> 202 us
  starting transfers between devices: 0.59 us -> 33.5 us
  local copies, waits for them, and re-layouts: 34.7 us -> 20.5 us
  between operations: 14.4 us -> 1.4 us
  other arithmetic: 4.45 us -> 13.6 us
    psum x3 -> x0, waiting for transfers between devices: 323 us -> none  [the longest x1 122 us: shards(): gram_total, top_rows = lax.psum((gram_part, top_part), 'row')]
    ppermute x0 -> x19, waiting for transfers between devices: none -> 202 us  [the longest x11 131 us: psum_doubling(): value = value + lax.ppermute(value, axis, _xor_pairs(count, bit))]
    all_gather x2 -> x0, waiting for transfers between devices: 185 us -> none  [mirror(): gathered = lax.all_gather(row_piece, 'row', axis=0, tiled=True)]
    ppermute x0 -> x19, starting transfers between devices: none -> 33.5 us  [the longest x11 17.2 us: psum_doubling(): value = value + lax.ppermute(value, axis, _xor_pairs(count, bit))]
    reshape x1 -> x0, local copies, waits for them, and re-layouts: 20.4 us -> none  [mirror(): gathered.reshape(group_ratio, col_count, blocks, band_size, band_size)]
    another operation x0 -> x5, local copies, waits for them, and re-layouts: none -> 8.65 us  [the longest x4 7.93 us: mirror_tree(): jnp.stack([first, second]).reshape(2, blocks, band_size, row_piece.shape[1])]
    dot_general x6 -> x9, matrix products: 29.5 us -> 29 us  [matmul(): jnp.dot(left, right, precision=lax.Precision.HIGHEST, preferred_element_t...]
  transfers between devices with their start and end apart: 5 -> 19, of which waited for: 5 -> 16; matrix products, arithmetic and copies ran while one was open for 1% -> 5% of each run, Pallas kernels for 0% -> 23%
where the time goes in v2:
time: 441 us; the launch traced here: 432 us
  waiting for transfers between devices  202 us (46%)
  Pallas kernels  100 us (23%)
  matrix products  60.5 us (14%)
  starting transfers between devices  33.5 us (8%)
  local copies, waits for them, and re-layouts  20.5 us (5%)
  other arithmetic  13.6 us (3%)
    ppermute x11, waiting for transfers between devices, psum_doubling(): value = value + lax.ppermute(value, axis, _xor_pairs(count, bit))  131 us
    pallas_call x2, Pallas kernels, eliminate(): pl.pallas_call(_elim_kernel, grid=(count,), in_specs=[spec], out_specs=[s...  100 us
    ppermute x6, waiting for transfers between devices, mirror_tree(): received = lax.ppermute(piece, ('row', 'col'), pairs)  53.9 us
    dot_general x9, matrix products, matmul(): jnp.dot(left, right, precision=lax.Precision.HIGHEST, preferred_element_t...  29 us
    dot_general x4, matrix products, matmul_nt(): lax.dot_general(left, right, (((1,), (1,)), ((), ())), precision=lax.Prec...  25.2 us
    ppermute x11, starting transfers between devices, psum_doubling(): value = value + lax.ppermute(value, axis, _xor_pairs(count, bit))  17.2 us
    ppermute x2, waiting for transfers between devices, mirror_tree(): other = lax.ppermute(piece, 'row', _xor_pairs(row_count, col_count))  16.8 us
    ppermute x6, starting transfers between devices, mirror_tree(): received = lax.ppermute(piece, ('row', 'col'), pairs)  9.99 us
  transfers between devices with their start and end apart: 19, of which 16 were waited for; matrix products, arithmetic and copies ran while one was open for 5% of the time, Pallas kernels for 23%

profile of v2, /device:TPU:1, one launch (start us, length us, event | category | flops | bytes accessed | tf_op | source)
XLA Modules:
  0.0 432.0 jit_solution(12665200699485029622)
XLA Ops:
  0.6 3.6 fusion.21
  4.3 1.5 collective-permute-start
  5.8 1.5 collective-permute-done
  8.8 11.8 %collective-permute-done.1 = f32[512,256]{1,0:T(8,128)S(1)} collective-permute-done((f32[512,256]{1,0:T(8,128)S(1)}, f32[512,256]{1,0:T(8,128)S(1)}, u32[]{:S(2)}, u32[]{:S(2)}) %collective-permute-start.1) | collective-permute-done | bytes 524320 | tf_op jit(solution)/shard_map/ppermute | solution.py:92
  20.6 1.5 collective-permute-start.2
  22.1 10.8 %collective-permute-done.2 = f32[512,256]{1,0:T(8,128)S(1)} collective-permute-done((f32[512,256]{1,0:T(8,128)S(1)}, f32[512,256]{1,0:T(8,128)S(1)}, u32[]{:S(2)}, u32[]{:S(2)}) %collective-permute-start.2) | collective-permute-done | bytes 524320 | tf_op jit(solution)/shard_map/ppermute | solution.py:92
  33.1 3.1 collective-permute-start.3
  36.2 10.0 %collective-permute-done.3 = f32[512,256]{1,0:T(8,128)S(1)} collective-permute-done((f32[512,256]{1,0:T(8,128)S(1)}, f32[512,256]{1,0:T(8,128)S(1)}, u32[]{:S(2)}, u32[]{:S(2)}) %collective-permute-start.3) | collective-permute-done | bytes 524320 | tf_op jit(solution)/shard_map/ppermute | solution.py:92
  49.4 5.1 %collective-permute-done.4 = f32[1024,256]{0,1:T(8,128)} collective-permute-done((f32[1024,256]{0,1:T(8,128)S(1)}, f32[1024,256]{0,1:T(8,128)}, u32[]{:S(2)}, u32[]{:S(2)}) %collective-permute-start.4) | collective-permute-done | bytes 1048608 | tf_op jit(solution)/shard_map/ppermute | solution.py:113
  55.9 2.3 collective-permute-start.5
  58.2 21.2 %collective-permute-done.5 = f32[1024,256]{0,1:T(8,128)} collective-permute-done((f32[1024,256]{0,1:T(8,128)S(1)}, f32[1024,256]{0,1:T(8,128)}, u32[]{:S(2)}, u32[]{:S(2)}) %collective-permute-start.5) | collective-permute-done | bytes 1048608 | tf_op jit(solution)/shard_map/ppermute | solution.py:113
  79.5 2.3 collective-permute-start.6
  81.8 34.0 %shard_map.41 = (f32[1,256,256]{2,1,0:T(8,128)}, f32[1,256,256]{2,1,0:T(8,128)}) custom-call(f32[1,256,256]{2,1,0:T(8,128)} %bitcast.87), custom_call_target="tpu_custom_call" | custom-call | tf_op jit(solution)/shard_map/pallas_call | solution.py:74
  115.8 2.6 gather_fusion
  118.4 1.5 fusion.3
  120.9 3.5 collective-permute-start.7
  125.3 66.3 %shard_map.42 = (f32[2,256,256]{2,1,0:T(8,128)}, f32[2,256,256]{2,1,0:T(8,128)}) custom-call(f32[2,256,256]{2,1,0:T(8,128)} %pad_maximum_fusion.3.m_ref), custom_call_target="tpu_custom_call" | custom-call | tf_op jit(solution)/shard_map/pallas_call | solution.py:74
  192.6 2.3 gather_fusion.1
  195.0 1.7 fusion.14
  196.7 1.9 fusion.22
  199.7 2.4 broadcast_select_fusion.9
  202.1 1.6 copy.18
  206.3 1.8 fusion.23
  209.9 1.9 bitcast_add_fusion
  212.9 16.1 %convolution_bitcast_fusion = f32[1024,256]{0,1:T(8,128)S(1)} fusion(f32[2048,256]{1,0:T(8,128)S(1)} %constant_dynamic-update-slice_fusion, f32[1024,2048]{1,0:T(8,128)} %param.6), kind=kOutput, calls=%fused_computation.7 | convolution fusion | flops 6442450944 | bytes 11534336 | tf_op jit(solution)/shard_map/dot_general | solution.py:12
  230.4 24.3 %collective-permute-done.8 = f32[1024,256]{0,1:T(8,128)S(1)} collective-permute-done((f32[1024,256]{0,1:T(8,128)S(1)}, f32[1024,256]{0,1:T(8,128)S(1)}, u32[]{:S(2)}, u32[]{:S(2)}) %collective-permute-start.8) | collective-permute-done | bytes 1048608 | tf_op jit(solution)/shard_map/ppermute | solution.py:92
  254.9 4.6 %collective-permute-start.9 = (f32[1024,256]{0,1:T(8,128)S(1)}, f32[1024,256]{0,1:T(8,128)S(1)}, u32[]{:S(2)}, u32[]{:S(2)}) collective-permute-start(f32[1024,256]{0,1:T(8,128)S(1)} %add.93), channel_id=1, source_target_pairs={{0,2},{1,3},{2,0},{3,1},{4,6},{5,7},{6,4},{7,5},{8,10},{9,11},{10,... | collective-permute-start | bytes 3145736 | tf_op jit(solution)/shard_map/ppermute | solution.py:92
  259.4 22.1 %collective-permute-done.9 = f32[1024,256]{0,1:T(8,128)S(1)} collective-permute-done((f32[1024,256]{0,1:T(8,128)S(1)}, f32[1024,256]{0,1:T(8,128)S(1)}, u32[]{:S(2)}, u32[]{:S(2)}) %collective-permute-start.9) | collective-permute-done | bytes 1048608 | tf_op jit(solution)/shard_map/ppermute | solution.py:92
  281.8 24.2 %collective-permute-done.10 = f32[1024,256]{0,1:T(8,128)S(1)} collective-permute-done((f32[1024,256]{0,1:T(8,128)S(1)}, f32[1024,256]{0,1:T(8,128)S(1)}, u32[]{:S(2)}, u32[]{:S(2)}) %collective-permute-start.10) | collective-permute-done | bytes 1048608 | tf_op jit(solution)/shard_map/ppermute | solution.py:92
  307.4 5.0 %collective-permute-done.11 = f32[1024,256]{0,1:T(8,128)S(1)} collective-permute-done((f32[1024,256]{0,1:T(8,128)S(1)}, f32[1024,256]{0,1:T(8,128)S(1)}, u32[]{:S(2)}, u32[]{:S(2)}) %collective-permute-start.11) | collective-permute-done | bytes 1048608 | tf_op jit(solution)/shard_map/ppermute | solution.py:113
  314.0 22.6 %collective-permute-done.12 = f32[1024,256]{0,1:T(8,128)S(1)} collective-permute-done((f32[1024,256]{0,1:T(8,128)S(1)}, f32[1024,256]{0,1:T(8,128)S(1)}, u32[]{:S(2)}, u32[]{:S(2)}) %collective-permute-start.12) | collective-permute-done | bytes 1048608 | tf_op jit(solution)/shard_map/ppermute | solution.py:113
  336.8 1.5 collective-permute-start.13
  341.3 2.3 collective-permute-start.16
  343.6 6.3 %collective-permute-done.16 = f32[256,256]{1,0:T(8,128)S(1)} collective-permute-done((f32[256,256]{1,0:T(8,128)S(1)}, f32[256,256]{1,0:T(8,128)S(1)}, u32[]{:S(2)}, u32[]{:S(2)}) %collective-permute-start.16) | collective-permute-done | bytes 262176 | tf_op jit(solution)/shard_map/ppermute | solution.py:92
  351.3 14.6 %collective-permute-done.17 = f32[256,256]{1,0:T(8,128)S(1)} collective-permute-done((f32[256,256]{1,0:T(8,128)S(1)}, f32[256,256]{1,0:T(8,128)S(1)}, u32[]{:S(2)}, u32[]{:S(2)}) %collective-permute-start.17) | collective-permute-done | bytes 262176 | tf_op jit(solution)/shard_map/ppermute | solution.py:92
  366.6 2.9 collective-permute-start.14
  369.4 4.6 %collective-permute-done.18 = f32[256,256]{1,0:T(8,128)S(1)} collective-permute-done((f32[256,256]{1,0:T(8,128)S(1)}, f32[256,256]{1,0:T(8,128)S(1)}, u32[]{:S(2)}, u32[]{:S(2)}) %collective-permute-start.18) | collective-permute-done | bytes 262176 | tf_op jit(solution)/shard_map/ppermute | solution.py:92
  375.1 1.8 convolution_multiply_fusion.1
  376.9 2.8 convolution_subtract_fusion
  379.7 16.8 %collective-permute-done.14 = f32[1024,256]{0,1:T(8,128)S(1)} collective-permute-done((f32[1024,256]{0,1:T(8,128)S(1)}, f32[1024,256]{0,1:T(8,128)S(1)}, u32[]{:S(2)}, u32[]{:S(2)}) %collective-permute-start.14) | collective-permute-done | bytes 1048608 | tf_op jit(solution)/shard_map/ppermute | solution.py:120
  396.6 1.5 broadcast_select_fusion.7
  398.1 2.5 copy.20
  400.6 2.5 copy.21
  403.1 1.7 pad_maximum_fusion.1
  404.8 1.8 fusion.24
  406.7 1.8 fusion
  408.5 13.6 %fusion.27 = f32[1024,2048]{1,0:T(8,128)S(1)} fusion(f32[1024,256]{0,1:T(8,128)S(1)} %get-tuple-element.43, f32[2048,256]{1,0:T(8,128)S(1)} %fusion), kind=kOutput, calls=%fused_computation.64 | convolution fusion | flops 6442450944 | bytes 11534336 | tf_op jit(solution)/shard_map/dot_general | solution.py:26
  422.2 9.7 %subtract_subtract_fusion = f32[1024,2048]{1,0:T(8,128)} fusion(f32[1024,2048]{1,0:T(8,128)S(1)} %bitcast.78, f32[1024,2048]{1,0:T(8,128)S(1)} %fusion.27, f32[1024,256]{1,0:T(8,128)S(1)} %copy-done.3, f32[2048,256]{1,0:T(8,128)S(1)} %constant_dynamic-update-slice_fusion), kind=kOutput, calls=%fused_computation.2 | convolution fusion | flops 6446645248 | bytes 28311552 | tf_op jit(solution)/shard_map/dot_general | solution.py:26
  (79 shorter events, 26.9 us)
Async XLA Ops:
  0.6 3.6 copy-start
  4.3 3.0 collective-permute-start
  7.4 13.2 %collective-permute-start.1 = (f32[512,256]{1,0:T(8,128)S(1)}, f32[512,256]{1,0:T(8,128)S(1)}, u32[]{:S(2)}, u32[]{:S(2)}) collective-permute-start(f32[512,256]{1,0:T(8,128)S(1)} %fusion.20), channel_id=1, source_target_pairs={{0,16},{8,24},{16,0},{24,8},{32,48},{40,56},{48,32},{56,40},{64,80... | collective-permute-start | bytes 1572872 | tf_op jit(solution)/shard_map/ppermute | solution.py:92
  20.6 12.3 %collective-permute-start.2 = (f32[512,256]{1,0:T(8,128)S(1)}, f32[512,256]{1,0:T(8,128)S(1)}, u32[]{:S(2)}, u32[]{:S(2)}) collective-permute-start(f32[512,256]{1,0:T(8,128)S(1)} %add.84), channel_id=1, source_target_pairs={{0,32},{8,40},{16,48},{24,56},{32,0},{40,8},{48,16},{56,24},{64,96... | collective-permute-start | bytes 1572872 | tf_op jit(solution)/shard_map/ppermute | solution.py:92
  33.1 13.1 %collective-permute-start.3 = (f32[512,256]{1,0:T(8,128)S(1)}, f32[512,256]{1,0:T(8,128)S(1)}, u32[]{:S(2)}, u32[]{:S(2)}) collective-permute-start(f32[512,256]{1,0:T(8,128)S(1)} %add.85), channel_id=1, source_target_pairs={{0,64},{8,72},{16,80},{24,88},{32,96},{40,104},{48,112},{56,120},{... | collective-permute-start | bytes 1572872 | tf_op jit(solution)/shard_map/ppermute | solution.py:92
  46.2 0.8 copy-start.6
  48.1 6.4 %collective-permute-start.4 = (f32[1024,256]{0,1:T(8,128)S(1)}, f32[1024,256]{0,1:T(8,128)}, u32[]{:S(2)}, u32[]{:S(2)}) collective-permute-start(f32[1024,256]{0,1:T(8,128)S(1)} %copy.10), channel_id=1, source_target_pairs={{0,8},{64,72},{9,1},{73,65},{18,26},{82,90},{27,19},{91,83},{36,44... | collective-permute-start | bytes 3145736 | tf_op jit(solution)/shard_map/ppermute | solution.py:113
  55.9 23.5 %collective-permute-start.5 = (f32[1024,256]{0,1:T(8,128)S(1)}, f32[1024,256]{0,1:T(8,128)}, u32[]{:S(2)}, u32[]{:S(2)}) collective-permute-start(f32[1024,256]{0,1:T(8,128)S(1)} %broadcast_select_fusion.1), channel_id=1, source_target_pairs={{0,16},{8,24},{64,80},{72,88},{1,17},{9,25},{65,81},{73,89},{18,2}... | collective-permute-start | bytes 3145736 | tf_op jit(solution)/shard_map/ppermute | solution.py:113
  79.5 41.3 %collective-permute-start.6 = (f32[1024,256]{0,1:T(8,128)S(1)}, f32[1024,256]{0,1:T(8,128)}, u32[]{:S(2)}, u32[]{:S(2)}) collective-permute-start(f32[1024,256]{0,1:T(8,128)S(1)} %broadcast_select_fusion.3), channel_id=1, source_target_pairs={{0,32},{8,40},{16,48},{24,56},{64,96},{72,104},{80,112},{88,120},{... | collective-permute-start | bytes 3145736 | tf_op jit(solution)/shard_map/ppermute | solution.py:113
  120.8 3.7 copy-start.7
  120.9 74.1 %copy-start.10 = (f32[1,256,256]{2,1,0:T(8,128)S(1)}, f32[1,256,256]{2,1,0:T(8,128)}, u32[]{:S(2)}) copy-start(f32[1,256,256]{2,1,0:T(8,128)} %get-tuple-element.34) | copy-start | bytes 786436
  120.9 78.7 %collective-permute-start.7 = (f32[1024,256]{0,1:T(8,128)S(1)}, f32[1024,256]{0,1:T(8,128)}, u32[]{:S(2)}, u32[]{:S(2)}) collective-permute-start(f32[1024,256]{0,1:T(8,128)S(1)} %broadcast_select_fusion.5), channel_id=1, source_target_pairs={{0,64},{8,72},{16,80},{24,88},{32,96},{40,104},{48,112},{56,120},{... | collective-permute-start | bytes 3145736 | tf_op jit(solution)/shard_map/ppermute | solution.py:120
  198.6 1.0 copy-start.2
  229.0 25.8 %collective-permute-start.8 = (f32[1024,256]{0,1:T(8,128)S(1)}, f32[1024,256]{0,1:T(8,128)S(1)}, u32[]{:S(2)}, u32[]{:S(2)}) collective-permute-start(f32[1024,256]{0,1:T(8,128)S(1)} %convolution_bitcast_fusion), channel_id=1, source_target_pairs={{0,1},{1,0},{2,3},{3,2},{4,5},{5,4},{6,7},{7,6},{8,9},{9,8},{10,11... | collective-permute-start | bytes 3145736 | tf_op jit(solution)/shard_map/ppermute | solution.py:92
  254.9 26.6 %collective-permute-start.9 = (f32[1024,256]{0,1:T(8,128)S(1)}, f32[1024,256]{0,1:T(8,128)S(1)}, u32[]{:S(2)}, u32[]{:S(2)}) collective-permute-start(f32[1024,256]{0,1:T(8,128)S(1)} %add.93), channel_id=1, source_target_pairs={{0,2},{1,3},{2,0},{3,1},{4,6},{5,7},{6,4},{7,5},{8,10},{9,11},{10,... | collective-permute-start | bytes 3145736 | tf_op jit(solution)/shard_map/ppermute | solution.py:92
  281.7 24.3 %collective-permute-start.10 = (f32[1024,256]{0,1:T(8,128)S(1)}, f32[1024,256]{0,1:T(8,128)S(1)}, u32[]{:S(2)}, u32[]{:S(2)}) collective-permute-start(f32[1024,256]{0,1:T(8,128)S(1)} %add.94), channel_id=1, source_target_pairs={{0,4},{1,5},{2,6},{3,7},{4,0},{5,1},{6,2},{7,3},{8,12},{9,13},{10,... | collective-permute-start | bytes 3145736 | tf_op jit(solution)/shard_map/ppermute | solution.py:92
  306.1 6.3 %collective-permute-start.11 = (f32[1024,256]{0,1:T(8,128)S(1)}, f32[1024,256]{0,1:T(8,128)S(1)}, u32[]{:S(2)}, u32[]{:S(2)}) collective-permute-start(f32[1024,256]{0,1:T(8,128)S(1)} %add.95), channel_id=1, source_target_pairs={{0,8},{64,72},{9,1},{73,65},{18,26},{82,90},{27,19},{91,83},{36,44... | collective-permute-start | bytes 3145736 | tf_op jit(solution)/shard_map/ppermute | solution.py:113
  312.6 23.9 %collective-permute-start.12 = (f32[1024,256]{0,1:T(8,128)S(1)}, f32[1024,256]{0,1:T(8,128)S(1)}, u32[]{:S(2)}, u32[]{:S(2)}) collective-permute-start(f32[1024,256]{0,1:T(8,128)S(1)} %broadcast_select_fusion), channel_id=1, source_target_pairs={{0,16},{8,24},{64,80},{72,88},{1,17},{9,25},{65,81},{73,89},{18,2}... | collective-permute-start | bytes 3145736 | tf_op jit(solution)/shard_map/ppermute | solution.py:113
  336.8 13.3 %copy-start.1 = (f32[1,256,256]{2,1,0:T(8,128)S(1)}, f32[1,256,256]{2,1,0:T(8,128)}, u32[]{:S(2)}) copy-start(f32[1,256,256]{2,1,0:T(8,128)} %get-tuple-element.33) | copy-start | bytes 786436
  336.8 29.6 %collective-permute-start.13 = (f32[1024,256]{0,1:T(8,128)S(1)}, f32[1024,256]{0,1:T(8,128)S(1)}, u32[]{:S(2)}, u32[]{:S(2)}) collective-permute-start(f32[1024,256]{0,1:T(8,128)S(1)} %broadcast_select_fusion.2), channel_id=1, source_target_pairs={{0,32},{8,40},{16,48},{24,56},{64,96},{72,104},{80,112},{88,120},{... | collective-permute-start | bytes 3145736 | tf_op jit(solution)/shard_map/ppermute | solution.py:113
  338.3 12.6 %copy-start.8 = (f32[2,256,256]{2,1,0:T(8,128)S(1)}, f32[2,256,256]{2,1,0:T(8,128)}, u32[]{:S(2)}) copy-start(f32[2,256,256]{2,1,0:T(8,128)} %get-tuple-element.35) | copy-start | bytes 1572868
  338.3 12.6 %copy-start.9 = (f32[2,256,256]{2,1,0:T(8,128)S(1)}, f32[2,256,256]{2,1,0:T(8,128)}, u32[]{:S(2)}) copy-start(f32[2,256,256]{2,1,0:T(8,128)} %get-tuple-element.36) | copy-start | bytes 1572868
  339.3 2.0 collective-permute-start.15
  341.3 8.6 %collective-permute-start.16 = (f32[256,256]{1,0:T(8,128)S(1)}, f32[256,256]{1,0:T(8,128)S(1)}, u32[]{:S(2)}, u32[]{:S(2)}) collective-permute-start(f32[256,256]{1,0:T(8,128)S(1)} %add.98), channel_id=1, source_target_pairs={{0,16},{8,24},{16,0},{24,8},{32,48},{40,56},{48,32},{56,40},{64,80... | collective-permute-start | bytes 786440 | tf_op jit(solution)/shard_map/ppermute | solution.py:92
  350.0 15.9 %collective-permute-start.17 = (f32[256,256]{1,0:T(8,128)S(1)}, f32[256,256]{1,0:T(8,128)S(1)}, u32[]{:S(2)}, u32[]{:S(2)}) collective-permute-start(f32[256,256]{1,0:T(8,128)S(1)} %add.99), channel_id=1, source_target_pairs={{0,32},{8,40},{16,48},{24,56},{32,0},{40,8},{48,16},{56,24},{64,96... | collective-permute-start | bytes 786440 | tf_op jit(solution)/shard_map/ppermute | solution.py:92
  365.9 8.2 %collective-permute-start.18 = (f32[256,256]{1,0:T(8,128)S(1)}, f32[256,256]{1,0:T(8,128)S(1)}, u32[]{:S(2)}, u32[]{:S(2)}) collective-permute-start(f32[256,256]{1,0:T(8,128)S(1)} %add.100), channel_id=1, source_target_pairs={{0,64},{8,72},{16,80},{24,88},{32,96},{40,104},{48,112},{56,120},{... | collective-permute-start | bytes 786440 | tf_op jit(solution)/shard_map/ppermute | solution.py:92
  366.6 30.0 %collective-permute-start.14 = (f32[1024,256]{0,1:T(8,128)S(1)}, f32[1024,256]{0,1:T(8,128)S(1)}, u32[]{:S(2)}, u32[]{:S(2)}) collective-permute-start(f32[1024,256]{0,1:T(8,128)S(1)} %broadcast_select_fusion.4), channel_id=1, source_target_pairs={{0,64},{8,72},{16,80},{24,88},{32,96},{40,104},{48,112},{56,120},{... | collective-permute-start | bytes 3145736 | tf_op jit(solution)/shard_map/ppermute | solution.py:120
  375.1 4.6 %copy-start.4 = (f32[256,256]{1,0:T(8,128)}, f32[256,256]{1,0:T(8,128)S(1)}, u32[]{:S(2)}) copy-start(f32[256,256]{1,0:T(8,128)S(1)} %fusion.26) | copy-start | bytes 786436
  404.8 1.8 copy-start.5
  406.6 15.5 %slice-start = ((s8[8388608]{0:T(1024)(128)(4,1)}), s8[4194304]{0:T(1024)(128)(4,1)S(1)}, s32[]{:S(2)}) async-start(s8[8388608]{0:T(1024)(128)(4,1)} %bitcast.77), calls=%async_computation | async-start | bytes 8388608
  408.5 13.7 %slice-start.1 = ((s8[8388608]{0:T(1024)(128)(4,1)}), s8[4194304]{0:T(1024)(128)(4,1)S(1)}, s32[]{:S(2)}) async-start(s8[8388608]{0:T(1024)(128)(4,1)} %bitcast.77), calls=%async_computation.1 | async-start | bytes 8388608
  408.5 13.7 %copy-start.3 = (f32[1024,256]{1,0:T(8,128)S(1)}, f32[1024,256]{1,0:T(8,128)}, u32[]{:S(2)}) copy-start(f32[1024,256]{1,0:T(8,128)} %convolution_subtract_fusion) | copy-start | bytes 3145732

commit v3 on v2

--- a/solution.py
+++ b/solution.py
@@ -33,11 +33,12 @@
 
 
 def _elim_kernel(m_ref, f_ref, r_ref):
-    n = m_ref.shape[0]
+    count, n, _ = m_ref.shape
     f_ref[...] = m_ref[...]
     ri = lax.broadcasted_iota(jnp.int32, (n, n), 0)
     ci = lax.broadcasted_iota(jnp.int32, (n, n), 1)
-    r_ref[...] = jnp.where(ri == ci, 1.0, 0.0).astype(jnp.float32)
+    for b in range(count):
+        r_ref[b] = jnp.where(ri == ci, 1.0, 0.0).astype(jnp.float32)
     for chunk in range(n // _CHUNK):
         r0 = chunk * _CHUNK
         c0 = (r0 // 128) * 128
@@ -46,39 +47,49 @@
         nc = n - c0
 
         def step(j, carry, r0=r0, c0=c0, rc1=rc1, nr=nr, nc=nc):
-            f = f_ref[r0:, c0:]
             rows = lax.broadcasted_iota(jnp.int32, (nr, nc), 0) + r0
-            row_j = jnp.sum(jnp.where(rows[:_CHUNK] == j, f[:_CHUNK], 0.0), axis=0, keepdims=True)
             lanes = lax.broadcasted_iota(jnp.int32, (nr, nc), 1) + c0
             lanes_row = lax.broadcasted_iota(jnp.int32, (1, nc), 1) + c0
             rows_col = lax.broadcasted_iota(jnp.int32, (nr, 1), 0) + r0
-            col_j = jnp.sum(jnp.where(lanes == j, f, 0.0), axis=1, keepdims=True)
-            pivot = jnp.sum(jnp.where(lanes_row == j, row_j, 0.0), axis=1, keepdims=True)
-            mult = jnp.where(rows_col > j, col_j / pivot, 0.0)
-            upd = jnp.where(lanes_row > j, row_j, 0.0)
-            f = f - mult * upd
-            f = jnp.where((lanes == j) & (rows > j), mult, f)
-            f_ref[r0:, c0:] = f
-            r_now = r_ref[r0:, :rc1]
             r_rows = lax.broadcasted_iota(jnp.int32, (_CHUNK, rc1), 0) + r0
-            r_row = jnp.sum(jnp.where(r_rows == j, r_now[:_CHUNK], 0.0), axis=0, keepdims=True)
-            r_ref[r0:, :rc1] = r_now - mult * r_row
+            for b in range(count):
+                f = f_ref[b, r0:, c0:]
+                row_j = jnp.sum(jnp.where(rows[:_CHUNK] == j, f[:_CHUNK], 0.0), axis=0, keepdims=True)
+                col_j = jnp.sum(jnp.where(lanes == j, f, 0.0), axis=1, keepdims=True)
+                pivot = jnp.sum(jnp.where(lanes_row == j, row_j, 0.0), axis=1, keepdims=True)
+                mult = jnp.where(rows_col > j, col_j / pivot, 0.0)
+                upd = jnp.where(lanes_row > j, row_j, 0.0)
+                f = f - mult * upd
+                f = jnp.where((lanes == j) & (rows > j), mult, f)
+                f_ref[b, r0:, c0:] = f
+                r_now = r_ref[b, r0:, :rc1]
+                r_row = jnp.sum(jnp.where(r_rows == j, r_now[:_CHUNK], 0.0), axis=0, keepdims=True)
+                r_ref[b, r0:, :rc1] = r_now - mult * r_row
             return carry
 
         lax.fori_loop(r0, r0 + _CHUNK, step, 0)
 
 
 def eliminate(stack):
-    count, n, _ = stack.shape
-    spec = pl.BlockSpec((None, n, n), lambda b: (b, 0, 0))
     return pl.pallas_call(
         _elim_kernel,
-        grid=(count,),
-        in_specs=[spec],
-        out_specs=[spec, spec],
         out_shape=[jax.ShapeDtypeStruct(stack.shape, jnp.float32)] * 2,
         interpret=_INTERPRET,
     )(stack)
+
+
+def matmul_fast(left, right):
+    return jnp.dot(left, right, precision=lax.Precision.HIGH, preferred_element_type=jnp.float32)
+
+
+def matmul_nt_fast(left, right):
+    return lax.dot_general(
+        left,
+        right,
+        (((1,), (1,)), ((), ())),
+        precision=lax.Precision.HIGH,
+        preferred_element_type=jnp.float32,
+    )
 
 
 def _xor_pairs(count, bit):
@@ -92,6 +103,23 @@
         value = value + lax.ppermute(value, axis, _xor_pairs(count, bit))
         bit *= 2
     return value
+
+
+def psum_halving(value, axis, bits):
+    index = lax.axis_index(axis)
+    count = lax.axis_size(axis)
+    keep = value
+    for bit in bits:
+        half = keep.shape[0] // 2
+        upper = (index & bit) != 0
+        send = jnp.where(upper, keep[:half], keep[half:])
+        mine = jnp.where(upper, keep[half:], keep[:half])
+        keep = mine + lax.ppermute(send, axis, _xor_pairs(count, bit))
+    for bit in reversed(bits):
+        upper = (index & bit) != 0
+        other = lax.ppermute(keep, axis, _xor_pairs(count, bit))
+        keep = jnp.where(upper, jnp.concatenate([other, keep]), jnp.concatenate([keep, other]))
+    return keep
 
 
 def mirror_tree(row_piece, band_size):
@@ -163,13 +191,13 @@
     refl_rows = refl_rows.at[:band_size].add(upper_inverse * first_owner)
     refl_cols = matmul(panel_cols, right)
     refl_cols = refl_cols.at[:band_size].add(upper_inverse * first_col)
-    product_rows = psum_doubling(matmul(trailing, refl_cols), "col")
+    product_rows = psum_halving(matmul_fast(trailing, refl_cols), "col", (2, 1, 4))
     inner_gram = psum_doubling(matmul_tn(refl_rows, product_rows), "row")
     product_cols = mirror_tree(product_rows, band_size)
     middle = matmul(matmul(tri_factor.T, inner_gram), tri_factor)
     update_rows = matmul(product_rows, tri_factor) - 0.5 * matmul(refl_rows, middle)
     update_cols = matmul(product_cols, tri_factor) - 0.5 * matmul(refl_cols, middle)
-    updated = trailing - matmul_nt(refl_rows, update_cols) - matmul_nt(update_rows, refl_cols)
+    updated = trailing - matmul_nt_fast(refl_rows, update_cols) - matmul_nt_fast(update_rows, refl_cols)
     return (updated, -chol_t)
 
 

time: 441 us -> 389 us (0.88); the launches traced: 432 us -> 386 us
  Pallas kernels: 100 us -> 74.7 us
  waiting for transfers between devices: 202 us -> 181 us
  matrix products: 60.5 us -> 43.5 us
  starting transfers between devices: 33.5 us -> 45.2 us
    ppermute x11 -> x8, waiting for transfers between devices: 131 us -> 61.1 us  [psum_doubling(): value = value + lax.ppermute(value, axis, _xor_pairs(count, bit))]
    ppermute x0 -> x6, waiting for transfers between devices: none -> 46.5 us  [the longest x3 26.8 us: psum_halving(): keep = mine + lax.ppermute(send, axis, _xor_pairs(count, bit))]
    pallas_call x2, Pallas kernels: 100 us -> 74.7 us  [eliminate(): pl.pallas_call(_elim_kernel, out_shape=[jax.ShapeDtypeStruct(stack.shape,...]
    dot_general x4 -> x2, matrix products: 25.2 us -> 1.93 us  [matmul_nt(): lax.dot_general(left, right, (((1,), (1,)), ((), ())), precision=lax.Prec...]
    dot_general x0 -> x3, matrix products: none -> 22.3 us  [the longest x2 13.1 us: matmul_nt_fast(): lax.dot_general(left, right, (((1,), (1,)), ((), ())), precision=lax.Prec...]
    ppermute x0 -> x6, starting transfers between devices: none -> 18.1 us  [the longest x3 16.9 us: psum_halving(): keep = mine + lax.ppermute(send, axis, _xor_pairs(count, bit))]
    dot_general x9 -> x8, matrix products: 29 us -> 12.9 us  [matmul(): jnp.dot(left, right, precision=lax.Precision.HIGHEST, preferred_element_t...]
    ppermute x11 -> x8, starting transfers between devices: 17.2 us -> 11.5 us  [psum_doubling(): value = value + lax.ppermute(value, axis, _xor_pairs(count, bit))]
  transfers between devices with their start and end apart: 19 -> 22, of which waited for: 16 -> 19; matrix products, arithmetic and copies ran while one was open for 5% -> 5% of each run, Pallas kernels for 23% -> 19%
where the time goes in v3:
time: 389 us; the launch traced here: 386 us
  waiting for transfers between devices  181 us (47%)
  Pallas kernels  74.7 us (19%)
  starting transfers between devices  45.2 us (12%)
  matrix products  43.5 us (11%)
  local copies, waits for them, and re-layouts  22.3 us (6%)
  other arithmetic  17.6 us (5%)
    pallas_call x2, Pallas kernels, eliminate(): pl.pallas_call(_elim_kernel, out_shape=[jax.ShapeDtypeStruct(stack.shape,...  74.7 us
    ppermute x8, waiting for transfers between devices, psum_doubling(): value = value + lax.ppermute(value, axis, _xor_pairs(count, bit))  61.1 us
    ppermute x6, waiting for transfers between devices, mirror_tree(): received = lax.ppermute(piece, ('row', 'col'), pairs)  56.8 us
    ppermute x3, waiting for transfers between devices, psum_halving(): keep = mine + lax.ppermute(send, axis, _xor_pairs(count, bit))  26.8 us
    ppermute x3, waiting for transfers between devices, psum_halving(): other = lax.ppermute(keep, axis, _xor_pairs(count, bit))  19.7 us
    ppermute x3, starting transfers between devices, psum_halving(): keep = mine + lax.ppermute(send, axis, _xor_pairs(count, bit))  16.9 us
    ppermute x2, waiting for transfers between devices, mirror_tree(): other = lax.ppermute(piece, 'row', _xor_pairs(row_count, col_count))  16.8 us
    dot_general x2, matrix products, matmul_nt_fast(): lax.dot_general(left, right, (((1,), (1,)), ((), ())), precision=lax.Prec...  13.1 us
  transfers between devices with their start and end apart: 22, of which 19 were waited for; matrix products, arithmetic and copies ran while one was open for 5% of the time, Pallas kernels for 19%

profile of v3, /device:TPU:1, one launch (start us, length us, event | category | flops | bytes accessed | tf_op | source)
XLA Modules:
  0.0 385.8 jit_solution(2249531641217085705)
XLA Ops:
  0.6 3.6 fusion.21
  5.8 1.5 collective-permute-done
  8.8 11.8 %collective-permute-done.1 = f32[512,256]{1,0:T(8,128)S(1)} collective-permute-done((f32[512,256]{1,0:T(8,128)S(1)}, f32[512,256]{1,0:T(8,128)S(1)}, u32[]{:S(2)}, u32[]{:S(2)}) %collective-permute-start.1) | collective-permute-done | bytes 524320 | tf_op jit(solution)/shard_map/ppermute | solution.py:103
  22.1 10.8 %collective-permute-done.2 = f32[512,256]{1,0:T(8,128)S(1)} collective-permute-done((f32[512,256]{1,0:T(8,128)S(1)}, f32[512,256]{1,0:T(8,128)S(1)}, u32[]{:S(2)}, u32[]{:S(2)}) %collective-permute-start.2) | collective-permute-done | bytes 524320 | tf_op jit(solution)/shard_map/ppermute | solution.py:103
  33.1 3.1 collective-permute-start.3
  36.2 10.0 %collective-permute-done.3 = f32[512,256]{1,0:T(8,128)S(1)} collective-permute-done((f32[512,256]{1,0:T(8,128)S(1)}, f32[512,256]{1,0:T(8,128)S(1)}, u32[]{:S(2)}, u32[]{:S(2)}) %collective-permute-start.3) | collective-permute-done | bytes 524320 | tf_op jit(solution)/shard_map/ppermute | solution.py:103
  49.4 5.1 %collective-permute-done.4 = f32[1024,256]{0,1:T(8,128)} collective-permute-done((f32[1024,256]{0,1:T(8,128)S(1)}, f32[1024,256]{0,1:T(8,128)}, u32[]{:S(2)}, u32[]{:S(2)}) %collective-permute-start.4) | collective-permute-done | bytes 1048608 | tf_op jit(solution)/shard_map/ppermute | solution.py:141
  55.9 2.3 collective-permute-start.5
  58.2 21.2 %collective-permute-done.5 = f32[1024,256]{0,1:T(8,128)} collective-permute-done((f32[1024,256]{0,1:T(8,128)S(1)}, f32[1024,256]{0,1:T(8,128)}, u32[]{:S(2)}, u32[]{:S(2)}) %collective-permute-start.5) | collective-permute-done | bytes 1048608 | tf_op jit(solution)/shard_map/ppermute | solution.py:141
  79.5 2.3 collective-permute-start.6
  81.9 34.1 %shard_map.41 = (f32[1,256,256]{2,1,0:T(8,128)}, f32[1,256,256]{2,1,0:T(8,128)}) custom-call(f32[1,256,256]{2,1,0:T(8,128)} %bitcast.87), custom_call_target="tpu_custom_call" | custom-call | tf_op jit(solution)/shard_map/pallas_call | solution.py:74
  115.9 2.6 gather_fusion
  118.5 1.5 fusion.3
  121.1 3.3 collective-permute-start.7
  125.2 40.6 %shard_map.42 = (f32[2,256,256]{2,1,0:T(8,128)}, f32[2,256,256]{2,1,0:T(8,128)}) custom-call(f32[2,256,256]{2,1,0:T(8,128)} %pad_maximum_fusion.3.m_ref), custom_call_target="tpu_custom_call" | custom-call | tf_op jit(solution)/shard_map/pallas_call | solution.py:74
  166.9 2.3 gather_fusion.1
  169.2 1.7 fusion.14
  170.9 1.9 fusion.22
  173.9 2.4 broadcast_select_fusion.9
  176.2 1.6 copy.18
  180.5 1.8 fusion.23
  184.1 1.9 bitcast_add_fusion
  187.1 9.2 %convolution_bitcast_fusion = f32[1024,256]{0,1:T(8,128)S(1)} fusion(f32[2048,256]{1,0:T(8,128)S(1)} %constant_dynamic-update-slice_fusion, f32[1024,2048]{1,0:T(8,128)} %param.6), kind=kOutput, calls=%fused_computation.7 | convolution fusion | flops 3221225472 | bytes 11534336 | tf_op jit(solution)/shard_map/dot_general | solution.py:82
  198.2 16.8 %collective-permute-start.8 = (f32[512,256]{0,1:T(8,128)}, f32[512,256]{0,1:T(8,128)}, u32[]{:S(2)}, u32[]{:S(2)}) collective-permute-start(f32[512,256]{0,1:T(8,128)} %slice_select_fusion), channel_id=1, source_target_pairs={{0,2},{1,3},{2,0},{3,1},{4,6},{5,7},{6,4},{7,5},{8,10},{9,11},{10,... | collective-permute-start | bytes 1572872 | tf_op jit(solution)/shard_map/ppermute | solution.py:117
  215.1 12.6 %collective-permute-done.8 = f32[512,256]{0,1:T(8,128)} collective-permute-done((f32[512,256]{0,1:T(8,128)}, f32[512,256]{0,1:T(8,128)}, u32[]{:S(2)}, u32[]{:S(2)}) %collective-permute-start.8) | collective-permute-done | bytes 524320 | tf_op jit(solution)/shard_map/ppermute | solution.py:117
  227.6 1.5 select_add_fusion
  230.7 8.9 %collective-permute-done.9 = f32[256,256]{0,1:T(8,128)S(1)} collective-permute-done((f32[256,256]{0,1:T(8,128)}, f32[256,256]{0,1:T(8,128)S(1)}, u32[]{:S(2)}, u32[]{:S(2)}) %collective-permute-start.9) | collective-permute-done | bytes 262176 | tf_op jit(solution)/shard_map/ppermute | solution.py:117
  240.8 5.3 %collective-permute-done.10 = f32[128,256]{0,1:T(8,128)S(1)} collective-permute-done((f32[128,256]{0,1:T(8,128)S(1)}, f32[128,256]{0,1:T(8,128)S(1)}, u32[]{:S(2)}, u32[]{:S(2)}) %collective-permute-start.10) | collective-permute-done | bytes 131104 | tf_op jit(solution)/shard_map/ppermute | solution.py:117
  246.2 5.3 %collective-permute-done.11 = f32[128,256]{0,1:T(8,128)S(1)} collective-permute-done((f32[128,256]{0,1:T(8,128)S(1)}, f32[128,256]{0,1:T(8,128)S(1)}, u32[]{:S(2)}, u32[]{:S(2)}) %collective-permute-start.11) | collective-permute-done | bytes 131104 | tf_op jit(solution)/shard_map/ppermute | solution.py:120
  251.6 6.7 %collective-permute-done.12 = f32[256,256]{0,1:T(8,128)S(1)} collective-permute-done((f32[256,256]{0,1:T(8,128)S(1)}, f32[256,256]{0,1:T(8,128)S(1)}, u32[]{:S(2)}, u32[]{:S(2)}) %collective-permute-start.12) | collective-permute-done | bytes 262176 | tf_op jit(solution)/shard_map/ppermute | solution.py:120
  259.4 7.6 %collective-permute-done.13 = f32[512,256]{0,1:T(8,128)S(1)} collective-permute-done((f32[512,256]{0,1:T(8,128)S(1)}, f32[512,256]{0,1:T(8,128)S(1)}, u32[]{:S(2)}, u32[]{:S(2)}) %collective-permute-start.13) | collective-permute-done | bytes 524320 | tf_op jit(solution)/shard_map/ppermute | solution.py:120
  268.5 7.9 %collective-permute-done.14 = f32[1024,256]{0,1:T(8,128)S(1)} collective-permute-done((f32[1024,256]{0,1:T(8,128)S(1)}, f32[1024,256]{0,1:T(8,128)S(1)}, u32[]{:S(2)}, u32[]{:S(2)}) %collective-permute-start.14) | collective-permute-done | bytes 1048608 | tf_op jit(solution)/shard_map/ppermute | solution.py:141
  278.0 22.6 %collective-permute-done.15 = f32[1024,256]{0,1:T(8,128)S(1)} collective-permute-done((f32[1024,256]{0,1:T(8,128)S(1)}, f32[1024,256]{0,1:T(8,128)S(1)}, u32[]{:S(2)}, u32[]{:S(2)}) %collective-permute-start.15) | collective-permute-done | bytes 1048608 | tf_op jit(solution)/shard_map/ppermute | solution.py:141
  305.3 2.3 collective-permute-start.19
  307.6 6.3 %collective-permute-done.19 = f32[256,256]{1,0:T(8,128)S(1)} collective-permute-done((f32[256,256]{1,0:T(8,128)S(1)}, f32[256,256]{1,0:T(8,128)S(1)}, u32[]{:S(2)}, u32[]{:S(2)}) %collective-permute-start.19) | collective-permute-done | bytes 262176 | tf_op jit(solution)/shard_map/ppermute | solution.py:103
  315.3 14.6 %collective-permute-done.20 = f32[256,256]{1,0:T(8,128)S(1)} collective-permute-done((f32[256,256]{1,0:T(8,128)S(1)}, f32[256,256]{1,0:T(8,128)S(1)}, u32[]{:S(2)}, u32[]{:S(2)}) %collective-permute-start.20) | collective-permute-done | bytes 262176 | tf_op jit(solution)/shard_map/ppermute | solution.py:103
  330.9 2.3 collective-permute-start.17
  333.2 4.9 %collective-permute-done.21 = f32[256,256]{1,0:T(8,128)S(1)} collective-permute-done((f32[256,256]{1,0:T(8,128)S(1)}, f32[256,256]{1,0:T(8,128)S(1)}, u32[]{:S(2)}, u32[]{:S(2)}) %collective-permute-start.21) | collective-permute-done | bytes 262176 | tf_op jit(solution)/shard_map/ppermute | solution.py:103
  339.1 1.8 convolution_multiply_fusion.1
  340.9 2.9 convolution_subtract_fusion
  343.8 16.8 %collective-permute-done.17 = f32[1024,256]{0,1:T(8,128)S(1)} collective-permute-done((f32[1024,256]{0,1:T(8,128)S(1)}, f32[1024,256]{0,1:T(8,128)S(1)}, u32[]{:S(2)}, u32[]{:S(2)}) %collective-permute-start.17) | collective-permute-done | bytes 1048608 | tf_op jit(solution)/shard_map/ppermute | solution.py:148
  362.0 2.5 copy.20
  364.6 2.5 copy.21
  367.1 1.7 pad_maximum_fusion.1
  368.8 1.8 fusion.24
  370.6 1.8 fusion
  372.5 6.9 %fusion.27 = f32[1024,2048]{1,0:T(8,128)S(1)} fusion(f32[1024,256]{0,1:T(8,128)S(1)} %get-tuple-element.43, f32[2048,256]{1,0:T(8,128)S(1)} %fusion), kind=kOutput, calls=%fused_computation.73 | convolution fusion | flops 3221225472 | bytes 11534336 | tf_op jit(solution)/shard_map/dot_general | solution.py:86
  379.4 6.2 %subtract_subtract_fusion = f32[1024,2048]{1,0:T(8,128)} fusion(f32[1024,2048]{1,0:T(8,128)S(1)} %bitcast.78, f32[1024,2048]{1,0:T(8,128)S(1)} %fusion.27, f32[1024,256]{1,0:T(8,128)S(1)} %copy-done.5, f32[2048,256]{1,0:T(8,128)S(1)} %constant_dynamic-update-slice_fusion), kind=kOutput, calls=%fused_computation.2 | convolution fusion | flops 3225419776 | bytes 28311552 | tf_op jit(solution)/shard_map/dot_general | solution.py:86
  (99 shorter events, 37.3 us)
Async XLA Ops:
  0.6 3.6 copy-start
  4.3 3.0 collective-permute-start
  7.4 13.2 %collective-permute-start.1 = (f32[512,256]{1,0:T(8,128)S(1)}, f32[512,256]{1,0:T(8,128)S(1)}, u32[]{:S(2)}, u32[]{:S(2)}) collective-permute-start(f32[512,256]{1,0:T(8,128)S(1)} %fusion.20), channel_id=1, source_target_pairs={{0,16},{8,24},{16,0},{24,8},{32,48},{40,56},{48,32},{56,40},{64,80... | collective-permute-start | bytes 1572872 | tf_op jit(solution)/shard_map/ppermute | solution.py:103
  20.6 12.3 %collective-permute-start.2 = (f32[512,256]{1,0:T(8,128)S(1)}, f32[512,256]{1,0:T(8,128)S(1)}, u32[]{:S(2)}, u32[]{:S(2)}) collective-permute-start(f32[512,256]{1,0:T(8,128)S(1)} %add.84), channel_id=1, source_target_pairs={{0,32},{8,40},{16,48},{24,56},{32,0},{40,8},{48,16},{56,24},{64,96... | collective-permute-start | bytes 1572872 | tf_op jit(solution)/shard_map/ppermute | solution.py:103
  33.1 13.1 %collective-permute-start.3 = (f32[512,256]{1,0:T(8,128)S(1)}, f32[512,256]{1,0:T(8,128)S(1)}, u32[]{:S(2)}, u32[]{:S(2)}) collective-permute-start(f32[512,256]{1,0:T(8,128)S(1)} %add.85), channel_id=1, source_target_pairs={{0,64},{8,72},{16,80},{24,88},{32,96},{40,104},{48,112},{56,120},{... | collective-permute-start | bytes 1572872 | tf_op jit(solution)/shard_map/ppermute | solution.py:103
  46.2 0.8 copy-start.8
  48.1 6.4 %collective-permute-start.4 = (f32[1024,256]{0,1:T(8,128)S(1)}, f32[1024,256]{0,1:T(8,128)}, u32[]{:S(2)}, u32[]{:S(2)}) collective-permute-start(f32[1024,256]{0,1:T(8,128)S(1)} %copy.10), channel_id=1, source_target_pairs={{0,8},{64,72},{9,1},{73,65},{18,26},{82,90},{27,19},{91,83},{36,44... | collective-permute-start | bytes 3145736 | tf_op jit(solution)/shard_map/ppermute | solution.py:141
  55.9 23.5 %collective-permute-start.5 = (f32[1024,256]{0,1:T(8,128)S(1)}, f32[1024,256]{0,1:T(8,128)}, u32[]{:S(2)}, u32[]{:S(2)}) collective-permute-start(f32[1024,256]{0,1:T(8,128)S(1)} %broadcast_select_fusion.1), channel_id=1, source_target_pairs={{0,16},{8,24},{64,80},{72,88},{1,17},{9,25},{65,81},{73,89},{18,2}... | collective-permute-start | bytes 3145736 | tf_op jit(solution)/shard_map/ppermute | solution.py:141
  79.5 41.3 %collective-permute-start.6 = (f32[1024,256]{0,1:T(8,128)S(1)}, f32[1024,256]{0,1:T(8,128)}, u32[]{:S(2)}, u32[]{:S(2)}) collective-permute-start(f32[1024,256]{0,1:T(8,128)S(1)} %broadcast_select_fusion.3), channel_id=1, source_target_pairs={{0,32},{8,40},{16,48},{24,56},{64,96},{72,104},{80,112},{88,120},{... | collective-permute-start | bytes 3145736 | tf_op jit(solution)/shard_map/ppermute | solution.py:141
  120.9 3.5 copy-start.11
  121.0 48.2 %copy-start.14 = (f32[1,256,256]{2,1,0:T(8,128)S(1)}, f32[1,256,256]{2,1,0:T(8,128)}, u32[]{:S(2)}) copy-start(f32[1,256,256]{2,1,0:T(8,128)} %get-tuple-element.34) | copy-start | bytes 786436
  121.1 52.8 %collective-permute-start.7 = (f32[1024,256]{0,1:T(8,128)S(1)}, f32[1024,256]{0,1:T(8,128)}, u32[]{:S(2)}, u32[]{:S(2)}) collective-permute-start(f32[1024,256]{0,1:T(8,128)S(1)} %broadcast_select_fusion.5), channel_id=1, source_target_pairs={{0,64},{8,72},{16,80},{24,88},{32,96},{40,104},{48,112},{56,120},{... | collective-permute-start | bytes 3145736 | tf_op jit(solution)/shard_map/ppermute | solution.py:148
  170.9 3.0 copy-start.9
  172.8 1.0 copy-start.3
  179.1 1.4 copy-start.10
  196.4 1.0 copy-start.1
  198.2 29.4 %collective-permute-start.8 = (f32[512,256]{0,1:T(8,128)}, f32[512,256]{0,1:T(8,128)}, u32[]{:S(2)}, u32[]{:S(2)}) collective-permute-start(f32[512,256]{0,1:T(8,128)} %slice_select_fusion), channel_id=1, source_target_pairs={{0,2},{1,3},{2,0},{3,1},{4,6},{5,7},{6,4},{7,5},{8,10},{9,11},{10,... | collective-permute-start | bytes 1572872 | tf_op jit(solution)/shard_map/ppermute | solution.py:117
  229.1 0.8 copy-start.4
  230.6 8.9 %collective-permute-start.9 = (f32[256,256]{0,1:T(8,128)}, f32[256,256]{0,1:T(8,128)S(1)}, u32[]{:S(2)}, u32[]{:S(2)}) collective-permute-start(f32[256,256]{0,1:T(8,128)} %slice_select_fusion.1), channel_id=1, source_target_pairs={{0,1},{1,0},{2,3},{3,2},{4,5},{5,4},{6,7},{7,6},{8,9},{9,8},{10,11... | collective-permute-start | bytes 786440 | tf_op jit(solution)/shard_map/ppermute | solution.py:117
  240.7 5.4 %collective-permute-start.10 = (f32[128,256]{0,1:T(8,128)S(1)}, f32[128,256]{0,1:T(8,128)S(1)}, u32[]{:S(2)}, u32[]{:S(2)}) collective-permute-start(f32[128,256]{0,1:T(8,128)S(1)} %slice_select_fusion.2), channel_id=1, source_target_pairs={{0,4},{1,5},{2,6},{3,7},{4,0},{5,1},{6,2},{7,3},{8,12},{9,13},{10,... | collective-permute-start | bytes 393224 | tf_op jit(solution)/shard_map/ppermute | solution.py:117
  246.1 5.4 %collective-permute-start.11 = (f32[128,256]{0,1:T(8,128)S(1)}, f32[128,256]{0,1:T(8,128)S(1)}, u32[]{:S(2)}, u32[]{:S(2)}) collective-permute-start(f32[128,256]{0,1:T(8,128)S(1)} %select_add_fusion.2), channel_id=1, source_target_pairs={{0,4},{1,5},{2,6},{3,7},{4,0},{5,1},{6,2},{7,3},{8,12},{9,13},{10,... | collective-permute-start | bytes 393224 | tf_op jit(solution)/shard_map/ppermute | solution.py:120
  251.6 6.8 %collective-permute-start.12 = (f32[256,256]{0,1:T(8,128)S(1)}, f32[256,256]{0,1:T(8,128)S(1)}, u32[]{:S(2)}, u32[]{:S(2)}) collective-permute-start(f32[256,256]{0,1:T(8,128)S(1)} %maximum_select_fusion.2), channel_id=1, source_target_pairs={{0,1},{1,0},{2,3},{3,2},{4,5},{5,4},{6,7},{7,6},{8,9},{9,8},{10,11... | collective-permute-start | bytes 786440 | tf_op jit(solution)/shard_map/ppermute | solution.py:120
  258.4 8.6 %collective-permute-start.13 = (f32[512,256]{0,1:T(8,128)S(1)}, f32[512,256]{0,1:T(8,128)S(1)}, u32[]{:S(2)}, u32[]{:S(2)}) collective-permute-start(f32[512,256]{0,1:T(8,128)S(1)} %maximum_select_fusion.1), channel_id=1, source_target_pairs={{0,2},{1,3},{2,0},{3,1},{4,6},{5,7},{6,4},{7,5},{8,10},{9,11},{10,... | collective-permute-start | bytes 1572872 | tf_op jit(solution)/shard_map/ppermute | solution.py:120
  267.2 9.2 %collective-permute-start.14 = (f32[1024,256]{0,1:T(8,128)S(1)}, f32[1024,256]{0,1:T(8,128)S(1)}, u32[]{:S(2)}, u32[]{:S(2)}) collective-permute-start(f32[1024,256]{0,1:T(8,128)S(1)} %maximum_select_fusion), channel_id=1, source_target_pairs={{0,8},{64,72},{9,1},{73,65},{18,26},{82,90},{27,19},{91,83},{36,44... | collective-permute-start | bytes 3145736 | tf_op jit(solution)/shard_map/ppermute | solution.py:141
  276.6 23.9 %collective-permute-start.15 = (f32[1024,256]{0,1:T(8,128)S(1)}, f32[1024,256]{0,1:T(8,128)S(1)}, u32[]{:S(2)}, u32[]{:S(2)}) collective-permute-start(f32[1024,256]{0,1:T(8,128)S(1)} %broadcast_select_fusion), channel_id=1, source_target_pairs={{0,16},{8,24},{64,80},{72,88},{1,17},{9,25},{65,81},{73,89},{18,2}... | collective-permute-start | bytes 3145736 | tf_op jit(solution)/shard_map/ppermute | solution.py:141
  300.8 13.3 %copy-start.2 = (f32[1,256,256]{2,1,0:T(8,128)S(1)}, f32[1,256,256]{2,1,0:T(8,128)}, u32[]{:S(2)}) copy-start(f32[1,256,256]{2,1,0:T(8,128)} %get-tuple-element.33) | copy-start | bytes 786436
  300.8 30.0 %collective-permute-start.16 = (f32[1024,256]{0,1:T(8,128)S(1)}, f32[1024,256]{0,1:T(8,128)S(1)}, u32[]{:S(2)}, u32[]{:S(2)}) collective-permute-start(f32[1024,256]{0,1:T(8,128)S(1)} %broadcast_select_fusion.2), channel_id=1, source_target_pairs={{0,32},{8,40},{16,48},{24,56},{64,96},{72,104},{80,112},{88,120},{... | collective-permute-start | bytes 3145736 | tf_op jit(solution)/shard_map/ppermute | solution.py:141
  302.3 12.6 %copy-start.12 = (f32[2,256,256]{2,1,0:T(8,128)S(1)}, f32[2,256,256]{2,1,0:T(8,128)}, u32[]{:S(2)}) copy-start(f32[2,256,256]{2,1,0:T(8,128)} %get-tuple-element.35) | copy-start | bytes 1572868
  302.3 12.6 %copy-start.13 = (f32[2,256,256]{2,1,0:T(8,128)S(1)}, f32[2,256,256]{2,1,0:T(8,128)}, u32[]{:S(2)}) copy-start(f32[2,256,256]{2,1,0:T(8,128)} %get-tuple-element.36) | copy-start | bytes 1572868
  303.3 2.0 collective-permute-start.18
  305.3 8.6 %collective-permute-start.19 = (f32[256,256]{1,0:T(8,128)S(1)}, f32[256,256]{1,0:T(8,128)S(1)}, u32[]{:S(2)}, u32[]{:S(2)}) collective-permute-start(f32[256,256]{1,0:T(8,128)S(1)} %add.98), channel_id=1, source_target_pairs={{0,16},{8,24},{16,0},{24,8},{32,48},{40,56},{48,32},{56,40},{64,80... | collective-permute-start | bytes 786440 | tf_op jit(solution)/shard_map/ppermute | solution.py:103
  314.0 15.9 %collective-permute-start.20 = (f32[256,256]{1,0:T(8,128)S(1)}, f32[256,256]{1,0:T(8,128)S(1)}, u32[]{:S(2)}, u32[]{:S(2)}) collective-permute-start(f32[256,256]{1,0:T(8,128)S(1)} %add.99), channel_id=1, source_target_pairs={{0,32},{8,40},{16,48},{24,56},{32,0},{40,8},{48,16},{56,24},{64,96... | collective-permute-start | bytes 786440 | tf_op jit(solution)/shard_map/ppermute | solution.py:103
  329.9 8.2 %collective-permute-start.21 = (f32[256,256]{1,0:T(8,128)S(1)}, f32[256,256]{1,0:T(8,128)S(1)}, u32[]{:S(2)}, u32[]{:S(2)}) collective-permute-start(f32[256,256]{1,0:T(8,128)S(1)} %add.100), channel_id=1, source_target_pairs={{0,64},{8,72},{16,80},{24,88},{32,96},{40,104},{48,112},{56,120},{... | collective-permute-start | bytes 786440 | tf_op jit(solution)/shard_map/ppermute | solution.py:103
  330.9 29.6 %collective-permute-start.17 = (f32[1024,256]{0,1:T(8,128)S(1)}, f32[1024,256]{0,1:T(8,128)S(1)}, u32[]{:S(2)}, u32[]{:S(2)}) collective-permute-start(f32[1024,256]{0,1:T(8,128)S(1)} %broadcast_select_fusion.4), channel_id=1, source_target_pairs={{0,64},{8,72},{16,80},{24,88},{32,96},{40,104},{48,112},{56,120},{... | collective-permute-start | bytes 3145736 | tf_op jit(solution)/shard_map/ppermute | solution.py:148
  339.1 4.7 %copy-start.6 = (f32[256,256]{1,0:T(8,128)}, f32[256,256]{1,0:T(8,128)S(1)}, u32[]{:S(2)}) copy-start(f32[256,256]{1,0:T(8,128)S(1)} %fusion.26) | copy-start | bytes 786436
  368.8 1.8 copy-start.7
  370.6 8.8 %slice-start = ((s8[8388608]{0:T(1024)(128)(4,1)}), s8[4194304]{0:T(1024)(128)(4,1)S(1)}, s32[]{:S(2)}) async-start(s8[8388608]{0:T(1024)(128)(4,1)} %bitcast.77), calls=%async_computation | async-start | bytes 8388608
  372.4 7.0 %slice-start.1 = ((s8[8388608]{0:T(1024)(128)(4,1)}), s8[4194304]{0:T(1024)(128)(4,1)S(1)}, s32[]{:S(2)}) async-start(s8[8388608]{0:T(1024)(128)(4,1)} %bitcast.77), calls=%async_computation.1 | async-start | bytes 8388608
  372.5 7.0 %copy-start.5 = (f32[1024,256]{1,0:T(8,128)S(1)}, f32[1024,256]{1,0:T(8,128)}, u32[]{:S(2)}) copy-start(f32[1024,256]{1,0:T(8,128)} %convolution_subtract_fusion) | copy-start | bytes 3145732
